TPU v7x, 128 devices: a whole 4x4x4 slice. The times are simulated.
128 devices in a mesh: ctx: 8 (over y, core), req: 16 (over x, z).
Axes of the slice: x: 4, y: 4, z: 4, core: 2. Of those that a mesh axis runs over, the one named last changes fastest.
Arguments:
- queries: bfloat16 [16, 512, 1024], P('req', 'ctx'), may hold values from -6 to 6
- keys: bfloat16 [16, 512, 1024], P('req', 'ctx'), may hold values from -6 to 6
- values: bfloat16 [16, 512, 2048], P('req', 'ctx'), may hold values from -6 to 6
- gate_input: bfloat16 [16, 512, 2048], P('req', 'ctx'), may hold values from -6 to 6
- beta: float32 [16, 16, 512], P('req', None, 'ctx'), may hold values from 0.05 to 1
- log_decay: float32 [16, 16, 512], P('req', None, 'ctx'), may hold values from -1 to 0
- norm_gain: float32 [128], replicated, may hold values from 0.1 to 1.9
- w_out: bfloat16 [2048, 2048], replicated, may hold values from -0.125 to 0.125
- hidden: bfloat16 [16, 512, 2048], P('req', 'ctx'), may hold values from -6 to 6
- post_gain: float32 [2048], replicated, may hold values from 0.1 to 1.9
- routes: int32 [16, 512, 10], P('req', 'ctx'), may hold values from 0 to 255, all different within a row; in each aligned block of 64 rows (0 to 63, 64 to 127, ..., all dimensions but the last counted through in order) at most 3 rows name the same one
- route_scores: float32 [16, 512, 10], P('req', 'ctx'), may hold values from 0.1 to 1
- expert_gate_up: bfloat16 [256, 2048, 1024], P(('ctx', 'req')), may hold values from -0.125 to 0.125
- expert_down: bfloat16 [256, 512, 2048], P(('ctx', 'req')), may hold values from -0.25 to 0.25
- accepted: int32 [16], P('req'), may hold values from 1 to 512
Outputs:
- layer_out: bfloat16 [16, 512, 2048], P('req', 'ctx')
- final_state: float32 [16, 16, 128, 128], P('req', 'ctx')
Inputs may be any that keep to these rules, and one draw needn't show every extreme that they name: A position's routes name different experts. Among the 64 positions of one device, no expert is named by more than 3 routes, a bound that some block reaches.
All inputs are finite; a program needn't handle non-finite values.
Results may differ from a plain program's by a relative error of at most 0.008.
Values may be sent and summed in bfloat16 or wider, within the bound.
No kernel may reach another device: no remote copies, remote signals or barrier semaphores. Data moves between devices by JAX's collectives and lax.ppermute only.
A program may use at most 128 MiB of HBM per device.

v0:
```python
import jax
import jax.numpy as jnp
from jax import lax
from jax.sharding import PartitionSpec as P

D = 2048
HK = 8
HV = 16
DK = 128
DV = 128
FFE = 512
TOPK = 10
EXP_DEV = 2


def unit_rows(x):
    x = x.astype(jnp.float32)
    return x * lax.rsqrt(jnp.sum(x * x, axis=-1, keepdims=True) + 1e-06)


def unit_lower_inverse(lower):
    highest = lax.Precision.HIGHEST
    n = lower.shape[-1]
    rows = jnp.arange(n)[:, None]
    cols = jnp.arange(n)[None, :]
    first = (rows // 2 == cols // 2) & (rows % 2 == 1) & (cols % 2 == 0)
    inv = lax.optimization_barrier(jnp.eye(n, dtype=lower.dtype) - jnp.where(first, lower, 0.0))

    def level(i, inv):
        b = jnp.left_shift(jnp.int32(1), i)
        sel = (rows // (2 * b) == cols // (2 * b)) & ((rows // b) % 2 == 1) & ((cols // b) % 2 == 0)
        c = jnp.where(sel, lower, 0.0)
        mc = jnp.einsum("...ij,...jk->...ik", inv, c, precision=highest)
        return inv - jnp.einsum("...ij,...jk->...ik", mc, inv, precision=highest)

    inv = lax.fori_loop(1, n.bit_length() - 1, level, inv)
    return inv


def run_experts(arrived, expert_gate_up, expert_down):
    provider_rows, count, part, width = arrived.shape
    rows = arrived.transpose(1, 0, 2, 3).reshape(count, provider_rows * part, width)
    both = jnp.einsum("erd,edf->erf", rows, expert_gate_up, preferred_element_type=jnp.float32)
    inner = (jax.nn.silu(both[..., :FFE]) * both[..., FFE:]).astype(jnp.bfloat16)
    result = jnp.einsum(
        "erf,efd->erd", inner, expert_down, preferred_element_type=jnp.float32
    ).astype(jnp.bfloat16)
    return result.reshape(count, provider_rows, part, width).transpose(1, 0, 2, 3)


def shards(
    queries,
    keys,
    values,
    gate_input,
    beta,
    log_decay,
    norm_gain,
    w_out,
    hidden,
    post_gain,
    routes,
    route_scores,
    expert_gate_up,
    expert_down,
    accepted,
):
    highest = lax.Precision.HIGHEST
    seq = queries.shape[1]
    n_ctx = lax.axis_size("ctx")
    n_req = lax.axis_size("req")
    n_dev = n_ctx * n_req
    experts = EXP_DEV * n_dev
    cap = max(2, 3 * seq * TOPK // (2 * experts))
    kh_dev = HK // n_ctx
    hv_dev = HV // n_ctx
    qw = kh_dev * DK
    vw = hv_dev * DV

    rates_decay = (
        jnp.stack([beta[0], log_decay[0]]).reshape(2, n_ctx, hv_dev, seq).transpose(1, 0, 2, 3)
    )
    hi = lax.reduce_precision(rates_decay, exponent_bits=8, mantissa_bits=7)
    rest = rates_decay - hi
    mid = lax.reduce_precision(rest, exponent_bits=8, mantissa_bits=7)
    lo = lax.reduce_precision(rest - mid, exponent_bits=8, mantissa_bits=7)
    width = 2 * qw + vw
    parts = jnp.stack([hi, mid, lo], axis=1).astype(jnp.bfloat16).reshape(n_ctx, -1)
    extra = -(-parts.shape[-1] // width)
    parts = jnp.pad(parts, ((0, 0), (0, extra * width - parts.shape[-1]))).reshape(n_ctx, extra, width)
    packed = jnp.concatenate(
        [
            jnp.concatenate(
                [
                    queries[0].reshape(seq, n_ctx, qw),
                    keys[0].reshape(seq, n_ctx, qw),
                    values[0].reshape(seq, n_ctx, vw),
                ],
                axis=2,
            ).transpose(1, 0, 2),
            parts,
        ],
        axis=1,
    )
    got = lax.all_to_all(packed, "ctx", 0, 0, tiled=True)
    arrived = got[:, :seq]
    rd = (
        got[:, seq:]
        .reshape(n_ctx, -1)[:, : 3 * 2 * hv_dev * seq]
        .astype(jnp.float32)
        .reshape(n_ctx, 3, 2, hv_dev, seq)
    )
    rd = (rd[:, 0] + rd[:, 1]) + rd[:, 2]
    rates = rd[:, 0].transpose(1, 0, 2)
    gamma = jnp.cumsum(rd[:, 1].transpose(1, 0, 2), axis=-1)
    qc = unit_rows(arrived[..., :qw]) * DK ** (-0.5)
    kc = unit_rows(arrived[..., qw : 2 * qw])
    vc = (
        arrived[..., 2 * qw : 2 * qw + vw]
        .astype(jnp.float32)
        .reshape(n_ctx, seq, hv_dev, DV)
        .transpose(2, 0, 1, 3)
    )

    ordinals = jnp.arange(seq)
    before = ordinals[:, None] > ordinals[None, :]
    upto = ordinals[:, None] >= ordinals[None, :]
    spans = gamma[..., :, None] - gamma[..., None, :]
    pair_decay = jnp.exp(jnp.where(upto, spans, 0.0))
    key_key = jnp.einsum("ntd,nsd->nts", kc, kc, precision=highest)
    lower = jnp.where(before, pair_decay * key_key[None] * rates[..., None, :], 0.0)
    inverse = unit_lower_inverse(lower)
    growth = jnp.exp(gamma)
    right = jnp.concatenate(
        [vc, growth[..., None] * jnp.broadcast_to(kc[None], vc.shape)], axis=-1
    )
    solved = jnp.einsum("hnts,hnsf->hntf", inverse, right, precision=highest)
    solved_values = solved[..., :DV]
    solved_keys = solved[..., DV:]
    tail = rates * jnp.exp(gamma[..., -1:] - gamma)
    weighted = (kc[None] * tail[..., None]).reshape(hv_dev * n_ctx, seq, DK)
    carried = jnp.einsum(
        "btd,btf->bdf", weighted, solved.reshape(hv_dev * n_ctx, seq, DV + DK), precision=highest
    ).reshape(hv_dev, n_ctx, DK, DV + DK)
    growth_last = growth[..., -1]
    key_part = carried[..., DV:]
    offset = carried[..., :DV]
    state = offset[:, 0]
    states = [jnp.zeros_like(state), state]
    for n in range(1, n_ctx - 1):
        state = (
            offset[:, n]
            + growth_last[:, n, None, None] * state
            - jnp.einsum("hde,hef->hdf", key_part[:, n], state, precision=highest)
        )
        states.append(state)
    states = jnp.stack(states, axis=1)
    pseudo = solved_values - jnp.einsum("hntd,hnde->hnte", solved_keys, states, precision=highest)
    query_key = jnp.einsum("ntd,nsd->nts", qc, kc, precision=highest)
    mixing = jnp.where(upto, pair_decay * query_key[None] * rates[..., None, :], 0.0)
    core = growth[..., None] * jnp.einsum("ntd,hnde->hnte", qc, states, precision=highest)
    core = core + jnp.einsum("hnts,hnse->hnte", mixing, pseudo, precision=highest)

    last = accepted[0] - 1
    chunk = last // seq
    local = last % seq
    gamma_chunk = lax.dynamic_index_in_dim(gamma, chunk, axis=1, keepdims=False)
    rates_chunk = lax.dynamic_index_in_dim(rates, chunk, axis=1, keepdims=False)
    pseudo_chunk = lax.dynamic_index_in_dim(pseudo, chunk, axis=1, keepdims=False)
    state_chunk = lax.dynamic_index_in_dim(states, chunk, axis=1, keepdims=False)
    keys_chunk = lax.dynamic_index_in_dim(kc, chunk, axis=0, keepdims=False)
    gamma_at = lax.dynamic_index_in_dim(gamma_chunk, local, axis=1, keepdims=False)
    keep = jnp.where(
        ordinals[None, :] <= local,
        rates_chunk * jnp.exp(jnp.minimum(gamma_at[:, None] - gamma_chunk, 0.0)),
        0.0,
    )
    final_state = jnp.exp(gamma_at)[:, None, None] * state_chunk + jnp.einsum(
        "td,hte->hde", keys_chunk, keep[..., None] * pseudo_chunk, precision=highest
    )
    final_state = final_state[None]

    scale = lax.rsqrt(jnp.mean(core * core, axis=-1, keepdims=True) + 1e-06)
    shaped = (core * scale * norm_gain).astype(jnp.bfloat16)
    shaped = shaped.transpose(1, 2, 0, 3).reshape(n_ctx, seq, vw)
    back = lax.all_to_all(shaped, "ctx", 0, 0, tiled=True)
    gating = jax.nn.silu(gate_input[0].astype(jnp.float32).reshape(seq, n_ctx, vw).transpose(1, 0, 2))
    normed = (back.astype(jnp.float32) * gating).astype(jnp.bfloat16)
    resid = hidden[0].astype(jnp.float32) + jnp.einsum(
        "jtf,jfd->td",
        normed,
        w_out.reshape(n_ctx, vw, D),
        preferred_element_type=jnp.float32,
    )
    moe_in = (
        resid * lax.rsqrt(jnp.mean(resid * resid, axis=-1, keepdims=True) + 1e-06) * post_gain
    ).astype(jnp.bfloat16)

    flat_ids = routes[0].reshape(-1)
    onehot = (flat_ids[:, None] == jnp.arange(experts, dtype=jnp.int32)[None, :]).astype(jnp.int32)
    earlier = jnp.cumsum(onehot, axis=0) - onehot
    slot = jnp.sum(earlier * onehot, axis=1)
    target = (flat_ids * cap + slot).reshape(seq, TOPK)
    slots = (
        jnp.arange(experts * cap, dtype=jnp.int32)
        .reshape(n_dev, EXP_DEV, cap)
        .transpose(0, 2, 1)
    )
    hits = target[None, None, None, :, :] == slots[..., None, None]
    dispatch = jnp.sum(jnp.where(hits, 1.0, 0.0), axis=-1).astype(jnp.bfloat16)
    outgoing_rows = jnp.einsum(
        "dcet,tf->dcef", dispatch, moe_in, preferred_element_type=jnp.float32
    ).astype(jnp.bfloat16)
    arrived_rows = lax.all_to_all(
        outgoing_rows, ("ctx", "req"), split_axis=0, concat_axis=0, tiled=True
    )
    both = jnp.einsum(
        "scex,exf->escf", arrived_rows, expert_gate_up, preferred_element_type=jnp.float32
    )
    inner = (jax.nn.silu(both[..., :FFE]) * both[..., FFE:]).astype(jnp.bfloat16)
    result = jnp.einsum(
        "escf,efx->scex", inner, expert_down, preferred_element_type=jnp.float32
    ).astype(jnp.bfloat16)
    returned = lax.all_to_all(result, ("ctx", "req"), split_axis=0, concat_axis=0, tiled=True)
    scores = route_scores[0]
    mix_weights = scores / jnp.sum(scores, axis=-1, keepdims=True)
    combine = jnp.sum(jnp.where(hits, mix_weights, 0.0), axis=-1)
    combine_hi = lax.reduce_precision(combine, exponent_bits=8, mantissa_bits=7)
    combine_lo = combine - combine_hi
    halves = jnp.concatenate([combine_hi, combine_lo], axis=-1).astype(jnp.bfloat16)
    both_out = jnp.einsum(
        "dcet,dcex->tx", halves, returned, preferred_element_type=jnp.float32
    )
    moe_out = both_out[:seq] + both_out[seq:]
    layer_out = (resid + moe_out).astype(jnp.bfloat16)[None]
    return (layer_out, final_state)


def solution(mesh):
    placed = (
        P("req", "ctx", None),
        P("req", "ctx", None),
        P("req", "ctx", None),
        P("req", "ctx", None),
        P("req", None, "ctx"),
        P("req", None, "ctx"),
        P(),
        P(),
        P("req", "ctx", None),
        P(),
        P("req", "ctx", None),
        P("req", "ctx", None),
        P(("ctx", "req"), None, None),
        P(("ctx", "req"), None, None),
        P("req"),
    )
    return jax.shard_map(
        shards,
        mesh=mesh,
        in_specs=placed,
        out_specs=(P("req", "ctx", None), P("req", "ctx", None, None)),
        check_vma=False,
    )
```

profile of v0, /device:TPU:1, one launch (start us, length us, event | category | flops | bytes accessed | tf_op | source)
XLA Modules:
  0.0 179.7 jit_solution(5321034913834717457)
XLA Ops:
  0.6 0.7 pad_maximum_fusion.2
  1.6 1.0 copy.291
  2.6 0.9 copy.289
  3.6 0.9 copy.290
  4.6 0.9 pad_maximum_fusion
  5.5 6.0 %all-to-all-start = ((bf16[8,66,512]{2,1,0:T(8,128)(2,1)}), bf16[8,66,512]{2,1,0:T(8,128)(2,1)S(1)}, u32[]{:S(2)}, u32[]{:S(2)}) async-start(bf16[8,66,512]{2,1,0:T(8,128)(2,1)} %pad_maximum_fusion), calls=%async_computation | async-start | bytes 1179648 | tf_op jit(solution)/shard_map/all_to_all | solution.py:105
  12.0 0.2 fusion.62
  12.3 0.2 copy.256
  12.5 0.3 fusion.66
  13.3 8.2 %all-to-all-done = bf16[8,66,512]{2,1,0:T(8,128)(2,1)S(1)} async-done(((bf16[8,66,512]{2,1,0:T(8,128)(2,1)}), bf16[8,66,512]{2,1,0:T(8,128)(2,1)S(1)}, u32[]{:S(2)}, u32[]{:S(2)}) %all-to-all-start) | async-done | bytes 540704 | tf_op jit(solution)/shard_map/all_to_all | solution.py:105
  21.7 0.5 reduce_window_sum.26
  22.1 0.2 fusion.87
  22.4 0.7 fusion.130
  23.2 0.2 slice_reduce_fusion.1
  23.3 0.2 select_subtract_fusion
  23.6 11.6 %while.18 = (s32[]{:T(128)}, f32[2,8,64,64]{3,2,1,0:T(8,128)S(1)}, f32[2,8,64]{2,1,0:T(8,128)S(1)}, pred[64,64]{0,1:T(8,128)(4,1)S(1)}, f32[8,64,64]{1,2,0:T(8,1...) while((s32[]{:T(128)}, f32[2,8,64,64]{3,2,1,0:T(8,128)S(1)}, ...), condition=%wide.region_3.4_spmd.clone.clone, body=%wide.region_2.3_spmd.clone.clone.sunk | while | flops 101137920 | bytes 1992085 | solution.py:36
  23.7 0.1 fusion.177
  24.0 1.2 fusion.178
  25.2 0.6 convolution_subtract_fusion.9
  26.3 1.2 fusion.178
  27.5 0.6 convolution_subtract_fusion.9
  28.3 0.1 fusion.177
  28.5 1.2 fusion.178
  29.8 0.6 convolution_subtract_fusion.9
  30.6 0.1 fusion.177
  30.8 1.2 fusion.178
  32.0 0.6 convolution_subtract_fusion.9
  33.1 1.2 fusion.178
  34.3 0.6 convolution_subtract_fusion.9
  35.2 0.2 slice_reduce_fusion
  35.4 0.1 convert_multiply_fusion.2
  35.5 0.2 broadcast_multiply_fusion
  35.7 0.2 bitcast_multiply_fusion.3
  35.9 0.3 slice_reduce_fusion.2
  36.3 1.0 fusion.57
  37.3 1.9 %fusion.151 = f32[16,128,256]{2,1,0:T(8,128)S(1)} fusion(f32[16,64,128]{2,1,0:T(8,128)S(1)} %bitcast_multiply_fusion.3, f32[16,64,256]{2,1,0:T(8,128)S(1)} %bitcast.369), kind=kOutput, calls=%fused_computation.267 | convolution fusion | flops 402653184 | bytes 3670016 | tf_op jit(solution)/shard_map/btd,btf->bdf/dot_general | solution.py:142
  39.2 0.3 bitcast_dynamic-update-slice_fusion.5
  39.5 0.3 bitcast_dynamic-update-slice_fusion.4
  39.8 0.3 bitcast_dynamic-update-slice_fusion.3
  40.0 0.3 bitcast_dynamic-update-slice_fusion.2
  40.3 0.3 bitcast_dynamic-update-slice_fusion.1
  40.6 0.3 fusion.54
  40.9 1.1 convolution_subtract_fusion.1
  42.0 0.8 fusion.92
  42.7 0.7 fusion.89
  43.4 1.0 fusion.76
  44.4 1.0 copy_bitcast_fusion
  45.5 4.3 %all-to-all-start.1 = ((bf16[8,64,256]{2,1,0:T(8,128)(2,1)}), bf16[8,64,256]{2,1,0:T(8,128)(2,1)S(1)}, u32[]{:S(2)}, u32[]{:S(2)}) async-start(bf16[8,64,256]{2,1,0:T(8,128)(2,1)} %copy_bitcast_fusion), calls=%async_computation.1 | async-start | bytes 524288 | tf_op jit(solution)/shard_map/all_to_all | solution.py:186
  49.9 0.4 fusion.50
  50.3 6.0 %all-to-all-done.1 = bf16[8,64,256]{2,1,0:T(8,128)(2,1)S(1)} async-done(((bf16[8,64,256]{2,1,0:T(8,128)(2,1)}), bf16[8,64,256]{2,1,0:T(8,128)(2,1)S(1)}, u32[]{:S(2)}, u32[]{:S(2)}) %all-to-all-start.1) | async-done | bytes 262176 | tf_op jit(solution)/shard_map/all_to_all | solution.py:186
  56.3 5.1 %multiply_reduce_fusion = (f32[64]{0:T(128)S(1)}, f32[64,2048]{1,0:T(8,128)S(1)}) fusion(bf16[8,256,2048]{2,1,0:T(8,128)(2,1)} %bitcast.368, f32[64,8,256]{2,1,0:T(8,128)S(1)} %bitcast.377, bf16[8,64,256]{2,1,0:T(8,128)(2,1)S(1)} %all-to-all-done.1, bf16[1,64,2048]{2,1,0:T(8,128)(2,1)} %param.25), kind=kOutput, calls=%fused_computation.120 | convolution fusion | flops 538312640 | bytes 9961728 | tf_op jit(solution)/shard_map/jtf,jfd->td/dot_general | solution.py:189
  61.4 1.0 convolution_convert_fusion
  62.5 3.2 %copy.259 = bf16[128,3,2,2048]{3,2,1,0:T(2,128)(2,1)S(1)} copy(bf16[128,3,2,2048]{3,0,1,2:T(8,128)(2,1)S(1)} %convolution_convert_fusion) | data formatting | bytes 6291456 | tf_op jit(solution)/shard_map/convert_element_type | solution.py:213
  65.7 49.7 %all_to_all.20 = bf16[128,3,2,2048]{3,2,1,0:T(2,128)(2,1)S(1)} all-to-all(bf16[128,3,2,2048]{3,2,1,0:T(2,128)(2,1)S(1)} %copy.259), channel_id=1, replica_groups=mesh['ctx'=8,'req'=16] {'ctx','req'}, dimensions={0} | all-to-all | bytes 6291456 | tf_op jit(solution)/shard_map/all_to_all | solution.py:214
  115.5 6.6 %fusion.33 = f32[2,128,3,1024]{3,1,2,0:T(8,128)S(1)} fusion(bf16[2,2048,1024]{2,1,0:T(8,128)(2,1)} %param.29, bf16[128,3,2,2048]{3,2,1,0:T(2,128)(2,1)S(1)} %all_to_all.20), kind=kOutput, calls=%fused_computation.51 | convolution fusion | flops 3221225472 | bytes 14680064 | tf_op jit(solution)/shard_map/scex,exf->escf/dot_general | solution.py:217
  122.1 1.9 %fusion.43 = bf16[128,3,2,2048]{3,0,2,1:T(8,128)(2,1)S(1)} fusion(bf16[2,512,2048]{2,1,0:T(8,128)(2,1)S(1)} %copy-done.5, f32[2,128,3,1024]{3,1,2,0:T(8,128)S(1)} %fusion.33), kind=kOutput, calls=%fused_computation.60 | convolution fusion | flops 1614544896 | bytes 10485760 | tf_op jit(solution)/shard_map/escf,efx->scex/dot_general | solution.py:221
  124.0 4.9 %copy.262 = bf16[128,3,2,2048]{3,2,1,0:T(2,128)(2,1)} copy(bf16[128,3,2,2048]{3,0,2,1:T(8,128)(2,1)S(1)} %fusion.43) | data formatting | bytes 6291456 | tf_op jit(solution)/shard_map/convert_element_type | solution.py:223
  128.9 5.3 %all-to-all-start.3 = ((bf16[128,3,2,2048]{3,2,1,0:T(2,128)(2,1)}), bf16[128,3,2,2048]{3,2,1,0:T(2,128)(2,1)}, u32[]{:S(2)}, u32[]{:S(2)}) async-start(bf16[128,3,2,2048]{3,2,1,0:T(2,128)(2,1)} %copy.262), calls=%async_computation.3 | async-start | bytes 6291456 | tf_op jit(solution)/shard_map/all_to_all | solution.py:224
  135.1 0.2 fusion.142
  135.4 0.5 fusion.56
  135.9 0.8 copy.265
  136.6 38.4 %all-to-all-done.3 = bf16[128,3,2,2048]{3,2,1,0:T(2,128)(2,1)} async-done(((bf16[128,3,2,2048]{3,2,1,0:T(2,128)(2,1)}), bf16[128,3,2,2048]{3,2,1,0:T(2,128)(2,1)}, u32[]{:S(2)}, u32[]{:S(2)}) %all-to-all-start.3) | async-done | bytes 3145760 | tf_op jit(solution)/shard_map/all_to_all | solution.py:224
  175.0 3.9 %fusion.46 = f32[128,2048]{1,0:T(8,128)S(1)} fusion(bf16[128,3,2,2048]{3,2,1,0:T(2,128)(2,1)} %all-to-all-done.3, bf16[128,3,2,64]{0,3,2,1:T(8,128)(2,1)S(1)} %get-tuple-element.332, bf16[128,3,2,64]{0,3,2,1:T(8,128)(2,1)S(1)} %get-tuple-element.331), kind=kOutput, calls=%fused_computation.63 | convolution fusion | flops 403046400 | bytes 4390912 | tf_op jit(solution)/shard_map/dcet,dcex->tx/dot_general | solution.py:231
  178.9 0.8 fusion.98
  (83 shorter events, 3.7 us)
Async XLA Ops:
  0.6 10.8 %copy-start.3 = (s32[1,64,10]{1,0,2:T(1,128)S(1)}, s32[1,64,10]{1,0,2:T(1,128)}, u32[]{:S(2)}) copy-start(s32[1,64,10]{1,0,2:T(1,128)} %param.27) | copy-start | bytes 7684
  5.5 16.0 %all-to-all-start = ((bf16[8,66,512]{2,1,0:T(8,128)(2,1)}), bf16[8,66,512]{2,1,0:T(8,128)(2,1)S(1)}, u32[]{:S(2)}, u32[]{:S(2)}) async-start(bf16[8,66,512]{2,1,0:T(8,128)(2,1)} %pad_maximum_fusion), calls=%async_computation | async-start | bytes 1179648 | tf_op jit(solution)/shard_map/all_to_all | solution.py:105
  11.4 1.8 %copy-start.1 = (f32[1,64,10]{1,0,2:T(1,128)S(1)}, f32[1,64,10]{1,0,2:T(1,128)}, u32[]{:S(2)}) copy-start(f32[1,64,10]{1,0,2:T(1,128)} %param.28) | copy-start | bytes 7684
  40.9 3.6 %copy-start.4 = (f32[128]{0:T(128)S(1)}, f32[128]{0:T(128)}, u32[]{:S(2)}) copy-start(f32[128]{0:T(128)} %param.23) | copy-start | bytes 1540
  41.9 7.8 %copy-start = (bf16[1,64,2048]{2,1,0:T(8,128)(2,1)S(1)}, bf16[1,64,2048]{2,1,0:T(8,128)(2,1)}, u32[]{:S(2)}) copy-start(bf16[1,64,2048]{2,1,0:T(8,128)(2,1)} %param.20) | copy-start | bytes 786436
  45.5 10.8 %all-to-all-start.1 = ((bf16[8,64,256]{2,1,0:T(8,128)(2,1)}), bf16[8,64,256]{2,1,0:T(8,128)(2,1)S(1)}, u32[]{:S(2)}, u32[]{:S(2)}) async-start(bf16[8,64,256]{2,1,0:T(8,128)(2,1)} %copy_bitcast_fusion), calls=%async_computation.1 | async-start | bytes 524288 | tf_op jit(solution)/shard_map/all_to_all | solution.py:186
  56.3 5.2 %copy-start.2 = (f32[2048]{0:T(1024)S(1)}, f32[2048]{0:T(1024)}, u32[]{:S(2)}) copy-start(f32[2048]{0:T(1024)} %param.26) | copy-start | bytes 24580
  115.5 6.7 %copy-start.5 = (bf16[2,512,2048]{2,1,0:T(8,128)(2,1)S(1)}, bf16[2,512,2048]{2,1,0:T(8,128)(2,1)}, u32[]{:S(2)}) copy-start(bf16[2,512,2048]{2,1,0:T(8,128)(2,1)} %param.30) | copy-start | bytes 12582916
  128.9 46.1 %all-to-all-start.3 = ((bf16[128,3,2,2048]{3,2,1,0:T(2,128)(2,1)}), bf16[128,3,2,2048]{3,2,1,0:T(2,128)(2,1)}, u32[]{:S(2)}, u32[]{:S(2)}) async-start(bf16[128,3,2,2048]{3,2,1,0:T(2,128)(2,1)} %copy.262), calls=%async_computation.3 | async-start | bytes 6291456 | tf_op jit(solution)/shard_map/all_to_all | solution.py:224
where the time goes:
time: 180 us
  waiting for transfers between devices  52.5 us (29%)
  blocking collectives  49.7 us (28%)
  matrix products  36.9 us (20%)
  starting transfers between devices  15.5 us (9%)
  local copies, waits for them, and re-layouts  14.5 us (8%)
  other arithmetic  8.12 us (5%)
  between operations  1.92 us (1%)
    all_to_all x1, blocking collectives, shards(): lax.all_to_all(outgoing_rows, ('ctx', 'req'), split_axis=0, concat_axis=0...  49.7 us
    all_to_all x1, waiting for transfers between devices, shards(): lax.all_to_all(result, ('ctx', 'req'), split_axis=0, concat_axis=0, tiled...  38.4 us
    all_to_all x1, waiting for transfers between devices, shards(): got = lax.all_to_all(packed, 'ctx', 0, 0, tiled=True)  8.18 us
    dot_general x1, matrix products, shards(): jnp.einsum('scex,exf->escf', arrived_rows, expert_gate_up, preferred_elem...  6.64 us
    dot_general x5, matrix products, level(): mc = jnp.einsum('...ij,...jk->...ik', inv, c, precision=highest)  6.02 us
    all_to_all x1, starting transfers between devices, shards(): got = lax.all_to_all(packed, 'ctx', 0, 0, tiled=True)  5.96 us
    all_to_all x1, waiting for transfers between devices, shards(): back = lax.all_to_all(shaped, 'ctx', 0, 0, tiled=True)  5.96 us
    all_to_all x1, starting transfers between devices, shards(): lax.all_to_all(result, ('ctx', 'req'), split_axis=0, concat_axis=0, tiled...  5.28 us
  transfers between devices with their start and end apart: 3, of which 3 were waited for; matrix products, arithmetic and copies ran while one was open for 2% of the time, Pallas kernels for 0%

commit v1 on v0

--- a/solution.py
+++ b/solution.py
@@ -186,11 +186,9 @@
     back = lax.all_to_all(shaped, "ctx", 0, 0, tiled=True)
     gating = jax.nn.silu(gate_input[0].astype(jnp.float32).reshape(seq, n_ctx, vw).transpose(1, 0, 2))
     normed = (back.astype(jnp.float32) * gating).astype(jnp.bfloat16)
-    resid = hidden[0].astype(jnp.float32) + jnp.einsum(
-        "jtf,jfd->td",
-        normed,
-        w_out.reshape(n_ctx, vw, D),
-        preferred_element_type=jnp.float32,
+    normed = normed.transpose(1, 0, 2).reshape(seq, HV * DV)
+    resid = hidden[0].astype(jnp.float32) + jnp.dot(
+        normed, w_out, preferred_element_type=jnp.float32
     )
     moe_in = (
         resid * lax.rsqrt(jnp.mean(resid * resid, axis=-1, keepdims=True) + 1e-06) * post_gain

time: 180 us -> 181 us (level)
  transfers between devices with their start and end apart: 3 -> 3, of which waited for: 3 -> 3; matrix products, arithmetic and copies ran while one was open for 2% -> 3% of each run, Pallas kernels for 0% -> 0%
where the time goes in v1:
time: 181 us; the launch traced here: 180 us
  waiting for transfers between devices  51.6 us (29%)
  blocking collectives  49.7 us (27%)
  matrix products  37 us (20%)
  local copies, waits for them, and re-layouts  15.5 us (9%)
  starting transfers between devices  15.5 us (9%)
  other arithmetic  8.35 us (5%)
  between operations  1.94 us (1%)
    all_to_all x1, blocking collectives, shards(): lax.all_to_all(outgoing_rows, ('ctx', 'req'), split_axis=0, concat_axis=0...  49.7 us
    all_to_all x1, waiting for transfers between devices, shards(): lax.all_to_all(result, ('ctx', 'req'), split_axis=0, concat_axis=0, tiled...  38.4 us
    all_to_all x1, waiting for transfers between devices, shards(): got = lax.all_to_all(packed, 'ctx', 0, 0, tiled=True)  8.18 us
    dot_general x1, matrix products, shards(): jnp.einsum('scex,exf->escf', arrived_rows, expert_gate_up, preferred_elem...  6.64 us
    dot_general x5, matrix products, level(): mc = jnp.einsum('...ij,...jk->...ik', inv, c, precision=highest)  6.02 us
    all_to_all x1, starting transfers between devices, shards(): got = lax.all_to_all(packed, 'ctx', 0, 0, tiled=True)  5.96 us
    all_to_all x1, starting transfers between devices, shards(): lax.all_to_all(result, ('ctx', 'req'), split_axis=0, concat_axis=0, tiled...  5.28 us
    dot_general x1, matrix products, shards(): jnp.dot(normed, w_out, preferred_element_type=jnp.float32)  5.09 us
  transfers between devices with their start and end apart: 3, of which 3 were waited for; matrix products, arithmetic and copies ran while one was open for 3% of the time, Pallas kernels for 0%

profile of v1, /device:TPU:1, one launch (start us, length us, event | category | flops | bytes accessed | tf_op | source)
XLA Modules:
  0.0 180.0 jit_solution(4747222953636930128)
XLA Ops:
  0.6 0.7 pad_maximum_fusion.2
  1.6 1.0 copy.295
  2.6 0.9 copy.293
  3.6 0.9 copy.294
  4.6 0.9 pad_maximum_fusion
  5.5 6.0 %all-to-all-start = ((bf16[8,66,512]{2,1,0:T(8,128)(2,1)}), bf16[8,66,512]{2,1,0:T(8,128)(2,1)S(1)}, u32[]{:S(2)}, u32[]{:S(2)}) async-start(bf16[8,66,512]{2,1,0:T(8,128)(2,1)} %pad_maximum_fusion), calls=%async_computation | async-start | bytes 1179648 | tf_op jit(solution)/shard_map/all_to_all | solution.py:105
  12.0 0.2 fusion.61
  12.3 0.2 copy.259
  12.5 0.3 fusion.65
  13.3 8.2 %all-to-all-done = bf16[8,66,512]{2,1,0:T(8,128)(2,1)S(1)} async-done(((bf16[8,66,512]{2,1,0:T(8,128)(2,1)}), bf16[8,66,512]{2,1,0:T(8,128)(2,1)S(1)}, u32[]{:S(2)}, u32[]{:S(2)}) %all-to-all-start) | async-done | bytes 540704 | tf_op jit(solution)/shard_map/all_to_all | solution.py:105
  21.7 0.5 reduce_window_sum.26
  22.1 0.2 fusion.86
  22.4 0.7 fusion.128
  23.2 0.2 slice_reduce_fusion.1
  23.3 0.2 select_subtract_fusion
  23.6 11.7 %while.18 = (s32[]{:T(128)}, f32[2,8,64,64]{3,2,1,0:T(8,128)S(1)}, f32[2,8,64]{2,1,0:T(8,128)S(1)}, pred[64,64]{0,1:T(8,128)(4,1)S(1)}, f32[8,64,64]{1,2,0:T(8,1...) while((s32[]{:T(128)}, f32[2,8,64,64]{3,2,1,0:T(8,128)S(1)}, ...), condition=%wide.region_3.4_spmd.clone.clone, body=%wide.region_2.3_spmd.clone.clone.sunk | while | flops 101137920 | bytes 1992085 | solution.py:36
  23.7 0.1 fusion.175
  24.0 1.2 fusion.176
  25.2 0.7 convolution_subtract_fusion.9
  26.3 1.2 fusion.176
  27.5 0.7 convolution_subtract_fusion.9
  28.6 1.2 fusion.176
  29.8 0.7 convolution_subtract_fusion.9
  30.9 1.2 fusion.176
  32.1 0.7 convolution_subtract_fusion.9
  33.2 1.2 fusion.176
  34.4 0.7 convolution_subtract_fusion.9
  35.3 0.2 slice_reduce_fusion
  35.4 0.1 convert_multiply_fusion.2
  35.6 0.2 broadcast_multiply_fusion
  35.8 0.2 bitcast_multiply_fusion.3
  36.0 0.3 slice_reduce_fusion.2
  36.3 1.0 fusion.56
  37.3 1.9 %fusion.148 = f32[16,128,256]{2,1,0:T(8,128)S(1)} fusion(f32[16,64,128]{2,1,0:T(8,128)S(1)} %bitcast_multiply_fusion.3, f32[16,64,256]{2,1,0:T(8,128)S(1)} %bitcast.367), kind=kOutput, calls=%fused_computation.265 | convolution fusion | flops 402653184 | bytes 3670016 | tf_op jit(solution)/shard_map/btd,btf->bdf/dot_general | solution.py:142
  39.3 0.3 bitcast_dynamic-update-slice_fusion.5
  39.5 0.3 bitcast_dynamic-update-slice_fusion.4
  39.8 0.3 bitcast_dynamic-update-slice_fusion.3
  40.1 0.3 bitcast_dynamic-update-slice_fusion.2
  40.4 0.3 bitcast_dynamic-update-slice_fusion.1
  40.6 0.3 fusion.53
  40.9 1.1 convolution_subtract_fusion.1
  42.0 0.8 fusion.91
  42.8 0.7 fusion.88
  43.5 1.0 fusion.75
  44.5 1.0 copy_bitcast_fusion
  45.6 4.3 %all-to-all-start.1 = ((bf16[8,64,256]{2,1,0:T(8,128)(2,1)}), bf16[8,64,256]{2,1,0:T(8,128)(2,1)S(1)}, u32[]{:S(2)}, u32[]{:S(2)}) async-start(bf16[8,64,256]{2,1,0:T(8,128)(2,1)} %copy_bitcast_fusion), calls=%async_computation.1 | async-start | bytes 524288 | tf_op jit(solution)/shard_map/all_to_all | solution.py:186
  49.9 1.0 copy.297
  51.0 0.4 fusion.49
  51.4 5.0 %all-to-all-done.1 = bf16[8,64,256]{2,1,0:T(8,128)(2,1)S(1)} async-done(((bf16[8,64,256]{2,1,0:T(8,128)(2,1)}), bf16[8,64,256]{2,1,0:T(8,128)(2,1)S(1)}, u32[]{:S(2)}, u32[]{:S(2)}) %all-to-all-start.1) | async-done | bytes 262176 | tf_op jit(solution)/shard_map/all_to_all | solution.py:186
  56.4 0.2 fusion.105
  56.7 5.1 %multiply_reduce_fusion = (f32[64]{0:T(128)S(1)}, f32[64,2048]{1,0:T(8,128)S(1)}) fusion(bf16[64,2048]{1,0:T(8,128)(2,1)S(1)} %bitcast.376, bf16[2048,2048]{1,0:T(8,128)(2,1)} %param.24, bf16[1,64,2048]{2,1,0:T(8,128)(2,1)S(1)} %copy-done), kind=kOutput, calls=%fused_computation.119 | convolution fusion | flops 537395136 | bytes 9437440 | tf_op jit(solution)/shard_map/dot_general | solution.py:190
  61.8 1.0 convolution_convert_fusion
  62.8 3.2 %copy.262 = bf16[128,3,2,2048]{3,2,1,0:T(2,128)(2,1)S(1)} copy(bf16[128,3,2,2048]{3,0,1,2:T(8,128)(2,1)S(1)} %convolution_convert_fusion) | data formatting | bytes 6291456 | tf_op jit(solution)/shard_map/convert_element_type | solution.py:211
  66.1 49.7 %all_to_all.20 = bf16[128,3,2,2048]{3,2,1,0:T(2,128)(2,1)S(1)} all-to-all(bf16[128,3,2,2048]{3,2,1,0:T(2,128)(2,1)S(1)} %copy.262), channel_id=1, replica_groups=mesh['ctx'=8,'req'=16] {'ctx','req'}, dimensions={0} | all-to-all | bytes 6291456 | tf_op jit(solution)/shard_map/all_to_all | solution.py:212
  115.8 6.6 %fusion.33 = f32[2,128,3,1024]{3,1,2,0:T(8,128)S(1)} fusion(bf16[2,2048,1024]{2,1,0:T(8,128)(2,1)} %param.29, bf16[128,3,2,2048]{3,2,1,0:T(2,128)(2,1)S(1)} %all_to_all.20), kind=kOutput, calls=%fused_computation.51 | convolution fusion | flops 3221225472 | bytes 14680064 | tf_op jit(solution)/shard_map/scex,exf->escf/dot_general | solution.py:215
  122.5 1.9 %fusion.43 = bf16[128,3,2,2048]{3,0,2,1:T(8,128)(2,1)S(1)} fusion(bf16[2,512,2048]{2,1,0:T(8,128)(2,1)S(1)} %copy-done.5, f32[2,128,3,1024]{3,1,2,0:T(8,128)S(1)} %fusion.33), kind=kOutput, calls=%fused_computation.60 | convolution fusion | flops 1614544896 | bytes 10485760 | tf_op jit(solution)/shard_map/escf,efx->scex/dot_general | solution.py:219
  124.3 4.9 %copy.265 = bf16[128,3,2,2048]{3,2,1,0:T(2,128)(2,1)} copy(bf16[128,3,2,2048]{3,0,2,1:T(8,128)(2,1)S(1)} %fusion.43) | data formatting | bytes 6291456 | tf_op jit(solution)/shard_map/convert_element_type | solution.py:221
  129.3 5.3 %all-to-all-start.3 = ((bf16[128,3,2,2048]{3,2,1,0:T(2,128)(2,1)}), bf16[128,3,2,2048]{3,2,1,0:T(2,128)(2,1)}, u32[]{:S(2)}, u32[]{:S(2)}) async-start(bf16[128,3,2,2048]{3,2,1,0:T(2,128)(2,1)} %copy.265), calls=%async_computation.3 | async-start | bytes 6291456 | tf_op jit(solution)/shard_map/all_to_all | solution.py:222
  135.4 0.2 fusion.140
  135.7 0.5 fusion.55
  136.2 0.8 copy.268
  136.9 38.4 %all-to-all-done.3 = bf16[128,3,2,2048]{3,2,1,0:T(2,128)(2,1)} async-done(((bf16[128,3,2,2048]{3,2,1,0:T(2,128)(2,1)}), bf16[128,3,2,2048]{3,2,1,0:T(2,128)(2,1)}, u32[]{:S(2)}, u32[]{:S(2)}) %all-to-all-start.3) | async-done | bytes 3145760 | tf_op jit(solution)/shard_map/all_to_all | solution.py:222
  175.3 3.9 %fusion.46 = f32[128,2048]{1,0:T(8,128)S(1)} fusion(bf16[128,3,2,2048]{3,2,1,0:T(2,128)(2,1)} %all-to-all-done.3, bf16[128,3,2,64]{0,3,2,1:T(8,128)(2,1)S(1)} %get-tuple-element.332, bf16[128,3,2,64]{0,3,2,1:T(8,128)(2,1)S(1)} %get-tuple-element.331), kind=kOutput, calls=%fused_computation.63 | convolution fusion | flops 403046400 | bytes 4390912 | tf_op jit(solution)/shard_map/dcet,dcex->tx/dot_general | solution.py:229
  179.2 0.8 fusion.96
  (85 shorter events, 4.0 us)
Async XLA Ops:
  0.6 10.8 %copy-start.3 = (s32[1,64,10]{1,0,2:T(1,128)S(1)}, s32[1,64,10]{1,0,2:T(1,128)}, u32[]{:S(2)}) copy-start(s32[1,64,10]{1,0,2:T(1,128)} %param.27) | copy-start | bytes 7684
  5.5 16.0 %all-to-all-start = ((bf16[8,66,512]{2,1,0:T(8,128)(2,1)}), bf16[8,66,512]{2,1,0:T(8,128)(2,1)S(1)}, u32[]{:S(2)}, u32[]{:S(2)}) async-start(bf16[8,66,512]{2,1,0:T(8,128)(2,1)} %pad_maximum_fusion), calls=%async_computation | async-start | bytes 1179648 | tf_op jit(solution)/shard_map/all_to_all | solution.py:105
  11.4 1.8 %copy-start.1 = (f32[1,64,10]{1,0,2:T(1,128)S(1)}, f32[1,64,10]{1,0,2:T(1,128)}, u32[]{:S(2)}) copy-start(f32[1,64,10]{1,0,2:T(1,128)} %param.28) | copy-start | bytes 7684
  40.9 3.6 %copy-start.4 = (f32[128]{0:T(128)S(1)}, f32[128]{0:T(128)}, u32[]{:S(2)}) copy-start(f32[128]{0:T(128)} %param.23) | copy-start | bytes 1540
  43.4 13.2 %copy-start = (bf16[1,64,2048]{2,1,0:T(8,128)(2,1)S(1)}, bf16[1,64,2048]{2,1,0:T(8,128)(2,1)}, u32[]{:S(2)}) copy-start(bf16[1,64,2048]{2,1,0:T(8,128)(2,1)} %param.25) | copy-start | bytes 786436
  45.6 10.8 %all-to-all-start.1 = ((bf16[8,64,256]{2,1,0:T(8,128)(2,1)}), bf16[8,64,256]{2,1,0:T(8,128)(2,1)S(1)}, u32[]{:S(2)}, u32[]{:S(2)}) async-start(bf16[8,64,256]{2,1,0:T(8,128)(2,1)} %copy_bitcast_fusion), calls=%async_computation.1 | async-start | bytes 524288 | tf_op jit(solution)/shard_map/all_to_all | solution.py:186
  56.6 5.1 %copy-start.2 = (f32[2048]{0:T(1024)S(1)}, f32[2048]{0:T(1024)}, u32[]{:S(2)}) copy-start(f32[2048]{0:T(1024)} %param.26) | copy-start | bytes 24580
  115.8 6.7 %copy-start.5 = (bf16[2,512,2048]{2,1,0:T(8,128)(2,1)S(1)}, bf16[2,512,2048]{2,1,0:T(8,128)(2,1)}, u32[]{:S(2)}) copy-start(bf16[2,512,2048]{2,1,0:T(8,128)(2,1)} %param.30) | copy-start | bytes 12582916
  129.3 46.1 %all-to-all-start.3 = ((bf16[128,3,2,2048]{3,2,1,0:T(2,128)(2,1)}), bf16[128,3,2,2048]{3,2,1,0:T(2,128)(2,1)}, u32[]{:S(2)}, u32[]{:S(2)}) async-start(bf16[128,3,2,2048]{3,2,1,0:T(2,128)(2,1)} %copy.265), calls=%async_computation.3 | async-start | bytes 6291456 | tf_op jit(solution)/shard_map/all_to_all | solution.py:222

commit v2 on v1

--- a/solution.py
+++ b/solution.py
@@ -97,12 +97,12 @@
                     values[0].reshape(seq, n_ctx, vw),
                 ],
                 axis=2,
-            ).transpose(1, 0, 2),
-            parts,
+            ),
+            parts.transpose(1, 0, 2),
         ],
-        axis=1,
-    )
-    got = lax.all_to_all(packed, "ctx", 0, 0, tiled=True)
+        axis=0,
+    )
+    got = lax.all_to_all(packed, "ctx", 1, 1, tiled=True).transpose(1, 0, 2)
     arrived = got[:, :seq]
     rd = (
         got[:, seq:]

time: 181 us -> 187 us (1.033)
  matrix products: 37 us -> 40.5 us
  other arithmetic: 8.35 us -> 10.8 us
  local copies, waits for them, and re-layouts: 15.5 us -> 17.6 us
  waiting for transfers between devices: 51.6 us -> 49.5 us
    dot_general x5, matrix products: 6.02 us -> 9.59 us  [level(): mc = jnp.einsum('...ij,...jk->...ik', inv, c, precision=highest)]
    all_to_all x1, waiting for transfers between devices: 8.18 us -> 5.83 us  [shards(): got = lax.all_to_all(packed, 'ctx', 1, 1, tiled=True).transpose(1, 0, 2)]
    unnamed x23 -> x45, local copies, waits for them, and re-layouts: 4.91 us -> 4.01 us
  transfers between devices with their start and end apart: 3 -> 3, of which waited for: 3 -> 3; matrix products, arithmetic and copies ran while one was open for 3% -> 4% of each run, Pallas kernels for 0% -> 0%
where the time goes in v2:
time: 187 us; the launch traced here: 186 us
  blocking collectives  49.7 us (27%)
  waiting for transfers between devices  49.5 us (26%)
  matrix products  40.5 us (22%)
  local copies, waits for them, and re-layouts  17.6 us (9%)
  starting transfers between devices  15.5 us (8%)
  other arithmetic  10.8 us (6%)
  between operations  2.01 us (1%)
    all_to_all x1, blocking collectives, shards(): lax.all_to_all(outgoing_rows, ('ctx', 'req'), split_axis=0, concat_axis=0...  49.7 us
    all_to_all x1, waiting for transfers between devices, shards(): lax.all_to_all(result, ('ctx', 'req'), split_axis=0, concat_axis=0, tiled...  37.7 us
    dot_general x5, matrix products, level(): mc = jnp.einsum('...ij,...jk->...ik', inv, c, precision=highest)  9.59 us
    dot_general x1, matrix products, shards(): jnp.einsum('scex,exf->escf', arrived_rows, expert_gate_up, preferred_elem...  6.65 us
    all_to_all x1, starting transfers between devices, shards(): got = lax.all_to_all(packed, 'ctx', 1, 1, tiled=True).transpose(1, 0, 2)  5.96 us
    all_to_all x1, waiting for transfers between devices, shards(): back = lax.all_to_all(shaped, 'ctx', 0, 0, tiled=True)  5.95 us
    all_to_all x1, waiting for transfers between devices, shards(): got = lax.all_to_all(packed, 'ctx', 1, 1, tiled=True).transpose(1, 0, 2)  5.83 us
    all_to_all x1, starting transfers between devices, shards(): lax.all_to_all(result, ('ctx', 'req'), split_axis=0, concat_axis=0, tiled...  5.28 us
  transfers between devices with their start and end apart: 3, of which 3 were waited for; matrix products, arithmetic and copies ran while one was open for 4% of the time, Pallas kernels for 0%

profile of v2, /device:TPU:1, one launch (start us, length us, event | category | flops | bytes accessed | tf_op | source)
XLA Modules:
  0.0 186.1 jit_solution(2915301359892989398)
XLA Ops:
  0.6 0.7 pad_maximum_fusion.2
  1.6 1.0 copy.295
  2.6 0.9 copy.293
  3.6 0.9 copy.294
  4.5 0.9 pad_maximum_fusion
  5.4 6.0 %all-to-all-start = ((bf16[66,8,512]{2,0,1:T(8,128)(2,1)}), bf16[66,8,512]{2,0,1:T(8,128)(2,1)S(1)}, u32[]{:S(2)}, u32[]{:S(2)}) async-start(bf16[66,8,512]{2,0,1:T(8,128)(2,1)} %pad_maximum_fusion), calls=%async_computation | async-start | bytes 1179648 | tf_op jit(solution)/shard_map/all_to_all | solution.py:105
  12.2 0.2 copy.259
  12.5 0.3 fusion.65
  12.7 0.7 and_and_fusion.1
  13.5 0.7 copy.232
  14.1 0.7 copy.231
  15.0 0.6 bitcast_divide_fusion
  15.6 5.8 %all-to-all-done = bf16[66,8,512]{2,0,1:T(8,128)(2,1)S(1)} async-done(((bf16[66,8,512]{2,0,1:T(8,128)(2,1)}), bf16[66,8,512]{2,0,1:T(8,128)(2,1)S(1)}, u32[]{:S(2)}, u32[]{:S(2)}) %all-to-all-start) | async-done | bytes 540704 | tf_op jit(solution)/shard_map/all_to_all | solution.py:105
  21.4 0.2 fusion.86
  21.7 0.6 add_rsqrt_fusion
  22.3 0.7 fusion.128
  23.3 0.6 fusion.147
  23.9 0.4 reduce_window_sum.26
  24.5 0.7 slice_reduce_fusion.1
  25.2 1.0 select_subtract_fusion
  26.2 15.2 %while.18 = (s32[]{:T(128)}, f32[2,8,64,64]{3,2,1,0:T(8,128)S(1)}, f32[2,8,64]{2,1,0:T(8,128)S(1)}, pred[64,64]{0,1:T(8,128)(4,1)}, f32[8,64,64]{1,2,0:T(8,128)S...) while((s32[]{:T(128)}, f32[2,8,64,64]{3,2,1,0:T(8,128)S(1)}, ...), condition=%wide.region_3.4_spmd.clone.clone, body=%wide.region_2.3_spmd.clone.clone.sunk | while | flops 101137920 | bytes 1992085 | solution.py:36
  26.6 1.9 %fusion.176 = f32[2,8,64,64]{2,3,1,0:T(8,128)S(1)} fusion(f32[2,8,64,64]{3,2,1,0:T(8,128)S(1)} %copy.355, f32[2,8,64]{2,1,0:T(8,128)S(1)} %get-tuple-element.439, f32[8,64,64]{1,2,0:T(8,128)S(1)} %get-tuple-element.438, f32[2,8,64]{2,1,0:T(8,128)S(1)} %get-tuple-element.436, pred[64,64]{0,1:T(8,128)(4,1)} %get-tuple-element.437, ...), kind=kOutput, calls=%fused_computation.7.clone.1 | convolution fusion | flops 50724864 | bytes 675840 | tf_op jit(solution)/shard_map/while/body/eval_jaxpr/...ij,...jk->...ik/dot_general | solution.py:33
  28.5 0.7 convolution_subtract_fusion.9
  29.6 1.9 %fusion.176 = f32[2,8,64,64]{2,3,1,0:T(8,128)S(1)} fusion(f32[2,8,64,64]{3,2,1,0:T(8,128)S(1)} %copy.355, f32[2,8,64]{2,1,0:T(8,128)S(1)} %get-tuple-element.439, f32[8,64,64]{1,2,0:T(8,128)S(1)} %get-tuple-element.438, f32[2,8,64]{2,1,0:T(8,128)S(1)} %get-tuple-element.436, pred[64,64]{0,1:T(8,128)(4,1)} %get-tuple-element.437, ...), kind=kOutput, calls=%fused_computation.7.clone.1 | convolution fusion | flops 50724864 | bytes 675840 | tf_op jit(solution)/shard_map/while/body/eval_jaxpr/...ij,...jk->...ik/dot_general | solution.py:33
  31.5 0.7 convolution_subtract_fusion.9
  32.6 1.9 %fusion.176 = f32[2,8,64,64]{2,3,1,0:T(8,128)S(1)} fusion(f32[2,8,64,64]{3,2,1,0:T(8,128)S(1)} %copy.355, f32[2,8,64]{2,1,0:T(8,128)S(1)} %get-tuple-element.439, f32[8,64,64]{1,2,0:T(8,128)S(1)} %get-tuple-element.438, f32[2,8,64]{2,1,0:T(8,128)S(1)} %get-tuple-element.436, pred[64,64]{0,1:T(8,128)(4,1)} %get-tuple-element.437, ...), kind=kOutput, calls=%fused_computation.7.clone.1 | convolution fusion | flops 50724864 | bytes 675840 | tf_op jit(solution)/shard_map/while/body/eval_jaxpr/...ij,...jk->...ik/dot_general | solution.py:33
  34.5 0.7 convolution_subtract_fusion.9
  35.6 1.9 %fusion.176 = f32[2,8,64,64]{2,3,1,0:T(8,128)S(1)} fusion(f32[2,8,64,64]{3,2,1,0:T(8,128)S(1)} %copy.355, f32[2,8,64]{2,1,0:T(8,128)S(1)} %get-tuple-element.439, f32[8,64,64]{1,2,0:T(8,128)S(1)} %get-tuple-element.438, f32[2,8,64]{2,1,0:T(8,128)S(1)} %get-tuple-element.436, pred[64,64]{0,1:T(8,128)(4,1)} %get-tuple-element.437, ...), kind=kOutput, calls=%fused_computation.7.clone.1 | convolution fusion | flops 50724864 | bytes 675840 | tf_op jit(solution)/shard_map/while/body/eval_jaxpr/...ij,...jk->...ik/dot_general | solution.py:33
  37.6 0.7 convolution_subtract_fusion.9
  38.6 1.9 %fusion.176 = f32[2,8,64,64]{2,3,1,0:T(8,128)S(1)} fusion(f32[2,8,64,64]{3,2,1,0:T(8,128)S(1)} %copy.355, f32[2,8,64]{2,1,0:T(8,128)S(1)} %get-tuple-element.439, f32[8,64,64]{1,2,0:T(8,128)S(1)} %get-tuple-element.438, f32[2,8,64]{2,1,0:T(8,128)S(1)} %get-tuple-element.436, pred[64,64]{0,1:T(8,128)(4,1)} %get-tuple-element.437, ...), kind=kOutput, calls=%fused_computation.7.clone.1 | convolution fusion | flops 50724864 | bytes 675840 | tf_op jit(solution)/shard_map/while/body/eval_jaxpr/...ij,...jk->...ik/dot_general | solution.py:33
  40.6 0.7 convolution_subtract_fusion.9
  41.7 0.2 broadcast_multiply_fusion
  42.1 0.3 slice_reduce_fusion.2
  42.3 1.0 fusion.56
  43.4 1.9 %fusion.148 = f32[16,128,256]{2,1,0:T(8,128)S(1)} fusion(f32[16,64,128]{2,1,0:T(8,128)S(1)} %bitcast_multiply_fusion.3, f32[16,64,256]{2,1,0:T(8,128)S(1)} %bitcast.369), kind=kOutput, calls=%fused_computation.265 | convolution fusion | flops 402653184 | bytes 3670016 | tf_op jit(solution)/shard_map/btd,btf->bdf/dot_general | solution.py:142
  45.3 0.3 bitcast_dynamic-update-slice_fusion.5
  45.6 0.3 bitcast_dynamic-update-slice_fusion.4
  45.8 0.3 bitcast_dynamic-update-slice_fusion.3
  46.1 0.3 bitcast_dynamic-update-slice_fusion.2
  46.4 0.3 bitcast_dynamic-update-slice_fusion.1
  46.7 0.3 fusion.53
  47.0 1.1 convolution_subtract_fusion.1
  48.1 0.8 fusion.91
  48.9 0.7 fusion.88
  49.5 1.0 fusion.75
  50.6 1.0 copy_bitcast_fusion
  51.7 4.3 %all-to-all-start.1 = ((bf16[8,64,256]{2,1,0:T(8,128)(2,1)}), bf16[8,64,256]{2,1,0:T(8,128)(2,1)S(1)}, u32[]{:S(2)}, u32[]{:S(2)}) async-start(bf16[8,64,256]{2,1,0:T(8,128)(2,1)} %copy_bitcast_fusion), calls=%async_computation.1 | async-start | bytes 524288 | tf_op jit(solution)/shard_map/all_to_all | solution.py:186
  56.1 0.4 fusion.49
  56.5 6.0 %all-to-all-done.1 = bf16[8,64,256]{2,1,0:T(8,128)(2,1)S(1)} async-done(((bf16[8,64,256]{2,1,0:T(8,128)(2,1)}), bf16[8,64,256]{2,1,0:T(8,128)(2,1)S(1)}, u32[]{:S(2)}, u32[]{:S(2)}) %all-to-all-start.1) | async-done | bytes 262176 | tf_op jit(solution)/shard_map/all_to_all | solution.py:186
  62.5 0.2 fusion.105
  62.8 5.1 %multiply_reduce_fusion = (f32[64]{0:T(128)S(1)}, f32[64,2048]{1,0:T(8,128)S(1)}) fusion(bf16[64,2048]{1,0:T(8,128)(2,1)S(1)} %bitcast.385, bf16[2048,2048]{1,0:T(8,128)(2,1)} %param.24, bf16[1,64,2048]{2,1,0:T(8,128)(2,1)S(1)} %copy-done), kind=kOutput, calls=%fused_computation.118 | convolution fusion | flops 537395136 | bytes 9437440 | tf_op jit(solution)/shard_map/dot_general | solution.py:190
  67.9 1.0 convolution_convert_fusion
  68.9 3.2 %copy.262 = bf16[128,3,2,2048]{3,2,1,0:T(2,128)(2,1)S(1)} copy(bf16[128,3,2,2048]{3,0,1,2:T(8,128)(2,1)S(1)} %convolution_convert_fusion) | data formatting | bytes 6291456 | tf_op jit(solution)/shard_map/convert_element_type | solution.py:211
  72.2 49.7 %all_to_all.20 = bf16[128,3,2,2048]{3,2,1,0:T(2,128)(2,1)S(1)} all-to-all(bf16[128,3,2,2048]{3,2,1,0:T(2,128)(2,1)S(1)} %copy.262), channel_id=1, replica_groups=mesh['ctx'=8,'req'=16] {'ctx','req'}, dimensions={0} | all-to-all | bytes 6291456 | tf_op jit(solution)/shard_map/all_to_all | solution.py:212
  121.9 6.6 %fusion.33 = f32[2,128,3,1024]{3,1,2,0:T(8,128)S(1)} fusion(bf16[2,2048,1024]{2,1,0:T(8,128)(2,1)} %param.29, bf16[128,3,2,2048]{3,2,1,0:T(2,128)(2,1)S(1)} %all_to_all.20), kind=kOutput, calls=%fused_computation.51 | convolution fusion | flops 3221225472 | bytes 14680064 | tf_op jit(solution)/shard_map/scex,exf->escf/dot_general | solution.py:215
  128.6 1.9 %fusion.43 = bf16[128,3,2,2048]{3,0,2,1:T(8,128)(2,1)S(1)} fusion(bf16[2,512,2048]{2,1,0:T(8,128)(2,1)S(1)} %copy-done.16, f32[2,128,3,1024]{3,1,2,0:T(8,128)S(1)} %fusion.33), kind=kOutput, calls=%fused_computation.60 | convolution fusion | flops 1614544896 | bytes 10485760 | tf_op jit(solution)/shard_map/escf,efx->scex/dot_general | solution.py:219
  130.4 4.9 %copy.265 = bf16[128,3,2,2048]{3,2,1,0:T(2,128)(2,1)} copy(bf16[128,3,2,2048]{3,0,2,1:T(8,128)(2,1)S(1)} %fusion.43) | data formatting | bytes 6291456 | tf_op jit(solution)/shard_map/convert_element_type | solution.py:221
  135.4 5.3 %all-to-all-start.3 = ((bf16[128,3,2,2048]{3,2,1,0:T(2,128)(2,1)}), bf16[128,3,2,2048]{3,2,1,0:T(2,128)(2,1)}, u32[]{:S(2)}, u32[]{:S(2)}) async-start(bf16[128,3,2,2048]{3,2,1,0:T(2,128)(2,1)} %copy.265), calls=%async_computation.3 | async-start | bytes 6291456 | tf_op jit(solution)/shard_map/all_to_all | solution.py:222
  141.7 0.7 constant_dynamic-slice_fusion.1
  142.5 0.5 fusion.55
  143.0 0.8 copy.268
  143.7 37.7 %all-to-all-done.3 = bf16[128,3,2,2048]{3,2,1,0:T(2,128)(2,1)} async-done(((bf16[128,3,2,2048]{3,2,1,0:T(2,128)(2,1)}), bf16[128,3,2,2048]{3,2,1,0:T(2,128)(2,1)}, u32[]{:S(2)}, u32[]{:S(2)}) %all-to-all-start.3) | async-done | bytes 3145760 | tf_op jit(solution)/shard_map/all_to_all | solution.py:222
  181.4 3.9 %fusion.46 = f32[128,2048]{1,0:T(8,128)S(1)} fusion(bf16[128,3,2,2048]{3,2,1,0:T(2,128)(2,1)} %all-to-all-done.3, bf16[128,3,2,64]{0,3,2,1:T(8,128)(2,1)S(1)} %get-tuple-element.332, bf16[128,3,2,64]{0,3,2,1:T(8,128)(2,1)S(1)} %get-tuple-element.331), kind=kOutput, calls=%fused_computation.63 | convolution fusion | flops 403046400 | bytes 4390912 | tf_op jit(solution)/shard_map/dcet,dcex->tx/dot_general | solution.py:229
  185.3 0.8 fusion.96
  (106 shorter events, 4.7 us)
Async XLA Ops:
  2.6 8.9 %copy-start.13 = (s32[1,64,10]{1,0,2:T(1,128)S(1)}, s32[1,64,10]{1,0,2:T(1,128)}, u32[]{:S(2)}) copy-start(s32[1,64,10]{1,0,2:T(1,128)} %param.27) | copy-start | bytes 7684
  5.4 16.0 %all-to-all-start = ((bf16[66,8,512]{2,0,1:T(8,128)(2,1)}), bf16[66,8,512]{2,0,1:T(8,128)(2,1)S(1)}, u32[]{:S(2)}, u32[]{:S(2)}) async-start(bf16[66,8,512]{2,0,1:T(8,128)(2,1)} %pad_maximum_fusion), calls=%async_computation | async-start | bytes 1179648 | tf_op jit(solution)/shard_map/all_to_all | solution.py:105
  12.2 2.8 %copy-start.11 = (f32[1,64,10]{1,0,2:T(1,128)S(1)}, f32[1,64,10]{1,0,2:T(1,128)}, u32[]{:S(2)}) copy-start(f32[1,64,10]{1,0,2:T(1,128)} %param.28) | copy-start | bytes 7684
  13.4 0.7 copy-start.9
  13.4 0.7 copy-start.10
  22.3 1.6 copy-start.5
  23.3 0.6 copy-start.2
  26.2 15.2 %copy-start.3 = (f32[8,2,2,64]{3,0,2,1:T(8,128)S(1)}, f32[8,2,2,64]{3,0,2,1:T(8,128)}, u32[]{:S(2)}) copy-start(f32[8,2,2,64]{3,0,2,1:T(8,128)} %copy-done.2) | copy-start | bytes 24580
  26.2 15.2 %copy-start.14 = (f32[2,8]{1,0:T(2,128)S(1)}, f32[2,8]{1,0:T(2,128)}, u32[]{:S(2)}) copy-start(f32[2,8]{1,0:T(2,128)} %slice_reduce_fusion.1) | copy-start | bytes 196
  45.8 2.2 %copy-start.7 = (f32[8,64]{1,0:T(8,128)S(1)}, f32[8,64]{1,0:T(8,128)}, u32[]{:S(2)}) copy-start(f32[8,64]{1,0:T(8,128)} %get-tuple-element.359) | copy-start | bytes 6148
  46.7 2.2 %copy-start.6 = (f32[8,64]{1,0:T(8,128)S(1)}, f32[8,64]{1,0:T(8,128)}, u32[]{:S(2)}) copy-start(f32[8,64]{1,0:T(8,128)} %copy-done.5) | copy-start | bytes 6148
  47.0 2.6 %copy-start.4 = (pred[64,64]{1,0:T(8,128)(4,1)S(1)}, pred[64,64]{1,0:T(8,128)(4,1)}, u32[]{:S(2)}) copy-start(pred[64,64]{1,0:T(8,128)(4,1)} %copy.232) | copy-start | bytes 12292
  48.0 2.6 %copy-start.15 = (f32[128]{0:T(128)S(1)}, f32[128]{0:T(128)}, u32[]{:S(2)}) copy-start(f32[128]{0:T(128)} %param.23) | copy-start | bytes 1540
  48.8 7.1 %copy-start.1 = (bf16[1,64,2048]{2,1,0:T(8,128)(2,1)S(1)}, bf16[1,64,2048]{2,1,0:T(8,128)(2,1)}, u32[]{:S(2)}) copy-start(bf16[1,64,2048]{2,1,0:T(8,128)(2,1)} %param.20) | copy-start | bytes 786436
  49.5 6.6 %copy-start.8 = (f32[64,10]{0,1:T(8,128)S(1)}, f32[64,10]{0,1:T(8,128)}, u32[]{:S(2)}) copy-start(f32[64,10]{0,1:T(8,128)} %bitcast_divide_fusion) | copy-start | bytes 7684
  50.6 12.1 %copy-start = (bf16[1,64,2048]{2,1,0:T(8,128)(2,1)S(1)}, bf16[1,64,2048]{2,1,0:T(8,128)(2,1)}, u32[]{:S(2)}) copy-start(bf16[1,64,2048]{2,1,0:T(8,128)(2,1)} %param.25) | copy-start | bytes 786436
  51.7 10.8 %all-to-all-start.1 = ((bf16[8,64,256]{2,1,0:T(8,128)(2,1)}), bf16[8,64,256]{2,1,0:T(8,128)(2,1)S(1)}, u32[]{:S(2)}, u32[]{:S(2)}) async-start(bf16[8,64,256]{2,1,0:T(8,128)(2,1)} %copy_bitcast_fusion), calls=%async_computation.1 | async-start | bytes 524288 | tf_op jit(solution)/shard_map/all_to_all | solution.py:186
  62.7 5.1 %copy-start.12 = (f32[2048]{0:T(1024)S(1)}, f32[2048]{0:T(1024)}, u32[]{:S(2)}) copy-start(f32[2048]{0:T(1024)} %param.26) | copy-start | bytes 24580
  121.9 6.7 %copy-start.16 = (bf16[2,512,2048]{2,1,0:T(8,128)(2,1)S(1)}, bf16[2,512,2048]{2,1,0:T(8,128)(2,1)}, u32[]{:S(2)}) copy-start(bf16[2,512,2048]{2,1,0:T(8,128)(2,1)} %param.30) | copy-start | bytes 12582916
  135.4 46.1 %all-to-all-start.3 = ((bf16[128,3,2,2048]{3,2,1,0:T(2,128)(2,1)}), bf16[128,3,2,2048]{3,2,1,0:T(2,128)(2,1)}, u32[]{:S(2)}, u32[]{:S(2)}) async-start(bf16[128,3,2,2048]{3,2,1,0:T(2,128)(2,1)} %copy.265), calls=%async_computation.3 | async-start | bytes 6291456 | tf_op jit(solution)/shard_map/all_to_all | solution.py:222

commit v3 on v0

--- a/solution.py
+++ b/solution.py
@@ -33,7 +33,13 @@
         mc = jnp.einsum("...ij,...jk->...ik", inv, c, precision=highest)
         return inv - jnp.einsum("...ij,...jk->...ik", mc, inv, precision=highest)
 
-    inv = lax.fori_loop(1, n.bit_length() - 1, level, inv)
+    levels = n.bit_length() - 1
+    start = 1 + (levels - 1) % 2
+    for i in range(1, start):
+        inv = level(i, inv)
+    inv = lax.fori_loop(
+        0, (levels - start) // 2, lambda j, m: level(start + 2 * j + 1, level(start + 2 * j, m)), inv
+    )
     return inv
 
 

time: 180 us -> 178 us (0.989)
    dot_general x5, matrix products: 6.02 us -> 4.18 us  [level(): mc = jnp.einsum('...ij,...jk->...ik', inv, c, precision=highest)]
    unnamed x23 -> x22, local copies, waits for them, and re-layouts: 3.96 us -> 3.83 us
where the time goes in v3:
time: 178 us; the launch traced here: 177 us
  waiting for transfers between devices  52.6 us (30%)
  blocking collectives  49.7 us (28%)
  matrix products  35.1 us (20%)
  starting transfers between devices  15.5 us (9%)
  local copies, waits for them, and re-layouts  14 us (8%)
  other arithmetic  7.87 us (4%)
  between operations  1.92 us (1%)
    all_to_all x1, blocking collectives, shards(): lax.all_to_all(outgoing_rows, ('ctx', 'req'), split_axis=0, concat_axis=0...  49.7 us
    all_to_all x1, waiting for transfers between devices, shards(): lax.all_to_all(result, ('ctx', 'req'), split_axis=0, concat_axis=0, tiled...  38.4 us
    all_to_all x1, waiting for transfers between devices, shards(): got = lax.all_to_all(packed, 'ctx', 0, 0, tiled=True)  8.29 us
    dot_general x1, matrix products, shards(): jnp.einsum('scex,exf->escf', arrived_rows, expert_gate_up, preferred_elem...  6.65 us
    all_to_all x1, starting transfers between devices, shards(): got = lax.all_to_all(packed, 'ctx', 0, 0, tiled=True)  5.96 us
    all_to_all x1, waiting for transfers between devices, shards(): back = lax.all_to_all(shaped, 'ctx', 0, 0, tiled=True)  5.96 us
    all_to_all x1, starting transfers between devices, shards(): lax.all_to_all(result, ('ctx', 'req'), split_axis=0, concat_axis=0, tiled...  5.27 us
    dot_general x1, matrix products, shards(): jnp.einsum('jtf,jfd->td', normed, w_out.reshape(n_ctx, vw, D), preferred_...  5.13 us
  transfers between devices with their start and end apart: 3, of which 3 were waited for; matrix products, arithmetic and copies ran while one was open for 2% of the time, Pallas kernels for 0%

profile of v3, /device:TPU:1, one launch (start us, length us, event | category | flops | bytes accessed | tf_op | source)
XLA Modules:
  0.0 177.1 jit_solution(17064184149884515745)
XLA Ops:
  0.6 0.7 pad_maximum_fusion.2
  1.6 1.0 copy.284
  2.6 0.9 copy.282
  3.6 0.9 copy.283
  4.6 0.9 pad_maximum_fusion
  5.5 6.0 %all-to-all-start = ((bf16[8,66,512]{2,1,0:T(8,128)(2,1)}), bf16[8,66,512]{2,1,0:T(8,128)(2,1)S(1)}, u32[]{:S(2)}, u32[]{:S(2)}) async-start(bf16[8,66,512]{2,1,0:T(8,128)(2,1)} %pad_maximum_fusion), calls=%async_computation | async-start | bytes 1179648 | tf_op jit(solution)/shard_map/all_to_all | solution.py:111
  12.0 0.2 fusion.79
  12.3 0.2 copy.248
  12.5 0.3 fusion.83
  13.2 8.3 %all-to-all-done = bf16[8,66,512]{2,1,0:T(8,128)(2,1)S(1)} async-done(((bf16[8,66,512]{2,1,0:T(8,128)(2,1)}), bf16[8,66,512]{2,1,0:T(8,128)(2,1)S(1)}, u32[]{:S(2)}, u32[]{:S(2)}) %all-to-all-start) | async-done | bytes 540704 | tf_op jit(solution)/shard_map/all_to_all | solution.py:111
  21.7 0.5 reduce_window_sum.26
  22.1 0.2 slice_reduce_fusion.1
  22.3 0.2 fusion.106
  22.5 0.7 fusion.157
  23.2 0.2 select_subtract_fusion
  23.4 0.8 fusion.102
  24.3 0.6 convolution_subtract_fusion.2
  24.9 7.7 %while.18 = (s32[]{:T(128)}, f32[2,8,64,64]{3,2,1,0:T(8,128)S(1)}, f32[2,8,64]{2,1,0:T(8,128)S(1)}, pred[64,64]{1,0:T(8,128)(4,1)S(1)}, f32[8,64,64]{2,1,0:T(8,1...) while((s32[]{:T(128)}, f32[2,8,64,64]{3,2,1,0:T(8,128)S(1)}, ...), condition=%wide.region_3.4_spmd.clone.clone, body=%wide.region_2.3_spmd.clone.clone.sunk | while | flops 202275840 | bytes 2935545 | solution.py:40
  25.1 0.1 fusion.224
  25.3 0.8 fusion.225
  26.1 0.6 convolution_subtract_fusion.12
  27.2 0.8 fusion.227
  28.0 0.6 convolution_subtract_fusion.13
  28.8 0.1 fusion.224
  29.0 0.8 fusion.225
  29.9 0.6 convolution_subtract_fusion.12
  30.7 0.1 fusion.226
  30.9 0.8 fusion.227
  31.7 0.6 convolution_subtract_fusion.13
  32.7 0.2 slice_reduce_fusion
  32.8 0.1 convert_multiply_fusion.2
  33.0 0.2 broadcast_multiply_fusion
  33.2 0.2 bitcast_multiply_fusion.3
  33.4 0.3 slice_reduce_fusion.2
  33.7 1.0 fusion.74
  34.7 1.9 %fusion.180 = f32[16,128,256]{2,1,0:T(8,128)S(1)} fusion(f32[16,64,128]{2,1,0:T(8,128)S(1)} %bitcast_multiply_fusion.3, f32[16,64,256]{2,1,0:T(8,128)S(1)} %bitcast.413), kind=kOutput, calls=%fused_computation.325 | convolution fusion | flops 402653184 | bytes 3670016 | tf_op jit(solution)/shard_map/btd,btf->bdf/dot_general | solution.py:148
  36.6 0.3 bitcast_dynamic-update-slice_fusion.5
  36.9 0.3 bitcast_dynamic-update-slice_fusion.4
  37.2 0.3 bitcast_dynamic-update-slice_fusion.3
  37.5 0.3 bitcast_dynamic-update-slice_fusion.2
  37.7 0.3 bitcast_dynamic-update-slice_fusion.1
  38.0 0.3 fusion.71
  38.3 1.1 convolution_subtract_fusion.3
  39.4 0.8 fusion.111
  40.2 0.7 fusion.108
  40.8 1.0 fusion.93
  41.9 1.0 copy_bitcast_fusion
  42.9 4.3 %all-to-all-start.1 = ((bf16[8,64,256]{2,1,0:T(8,128)(2,1)}), bf16[8,64,256]{2,1,0:T(8,128)(2,1)S(1)}, u32[]{:S(2)}, u32[]{:S(2)}) async-start(bf16[8,64,256]{2,1,0:T(8,128)(2,1)} %copy_bitcast_fusion), calls=%async_computation.1 | async-start | bytes 524288 | tf_op jit(solution)/shard_map/all_to_all | solution.py:192
  47.4 0.4 fusion.67
  47.7 6.0 %all-to-all-done.1 = bf16[8,64,256]{2,1,0:T(8,128)(2,1)S(1)} async-done(((bf16[8,64,256]{2,1,0:T(8,128)(2,1)}), bf16[8,64,256]{2,1,0:T(8,128)(2,1)S(1)}, u32[]{:S(2)}, u32[]{:S(2)}) %all-to-all-start.1) | async-done | bytes 262176 | tf_op jit(solution)/shard_map/all_to_all | solution.py:192
  53.7 5.1 %multiply_reduce_fusion = (f32[64]{0:T(128)S(1)}, f32[64,2048]{1,0:T(8,128)S(1)}) fusion(bf16[8,256,2048]{2,1,0:T(8,128)(2,1)} %bitcast.412, f32[64,8,256]{2,1,0:T(8,128)S(1)} %bitcast.421, bf16[8,64,256]{2,1,0:T(8,128)(2,1)S(1)} %all-to-all-done.1, bf16[1,64,2048]{2,1,0:T(8,128)(2,1)} %param.25), kind=kOutput, calls=%fused_computation.156 | convolution fusion | flops 538312640 | bytes 9961728 | tf_op jit(solution)/shard_map/jtf,jfd->td/dot_general | solution.py:195
  58.9 1.0 convolution_convert_fusion
  59.9 3.2 %copy.251 = bf16[128,3,2,2048]{3,2,1,0:T(2,128)(2,1)S(1)} copy(bf16[128,3,2,2048]{3,0,1,2:T(8,128)(2,1)S(1)} %convolution_convert_fusion) | data formatting | bytes 6291456 | tf_op jit(solution)/shard_map/convert_element_type | solution.py:219
  63.2 49.7 %all_to_all.20 = bf16[128,3,2,2048]{3,2,1,0:T(2,128)(2,1)S(1)} all-to-all(bf16[128,3,2,2048]{3,2,1,0:T(2,128)(2,1)S(1)} %copy.251), channel_id=1, replica_groups=mesh['ctx'=8,'req'=16] {'ctx','req'}, dimensions={0} | all-to-all | bytes 6291456 | tf_op jit(solution)/shard_map/all_to_all | solution.py:220
  112.9 6.6 %fusion.50 = f32[2,128,3,1024]{3,1,2,0:T(8,128)S(1)} fusion(bf16[2,2048,1024]{2,1,0:T(8,128)(2,1)} %param.29, bf16[128,3,2,2048]{3,2,1,0:T(2,128)(2,1)S(1)} %all_to_all.20), kind=kOutput, calls=%fused_computation.86 | convolution fusion | flops 3221225472 | bytes 14680064 | tf_op jit(solution)/shard_map/scex,exf->escf/dot_general | solution.py:223
  119.6 1.9 %fusion.60 = bf16[128,3,2,2048]{3,0,2,1:T(8,128)(2,1)S(1)} fusion(bf16[2,512,2048]{2,1,0:T(8,128)(2,1)S(1)} %copy-done.5, f32[2,128,3,1024]{3,1,2,0:T(8,128)S(1)} %fusion.50), kind=kOutput, calls=%fused_computation.95 | convolution fusion | flops 1614544896 | bytes 10485760 | tf_op jit(solution)/shard_map/escf,efx->scex/dot_general | solution.py:227
  121.4 4.9 %copy.254 = bf16[128,3,2,2048]{3,2,1,0:T(2,128)(2,1)} copy(bf16[128,3,2,2048]{3,0,2,1:T(8,128)(2,1)S(1)} %fusion.60) | data formatting | bytes 6291456 | tf_op jit(solution)/shard_map/convert_element_type | solution.py:229
  126.4 5.3 %all-to-all-start.3 = ((bf16[128,3,2,2048]{3,2,1,0:T(2,128)(2,1)}), bf16[128,3,2,2048]{3,2,1,0:T(2,128)(2,1)}, u32[]{:S(2)}, u32[]{:S(2)}) async-start(bf16[128,3,2,2048]{3,2,1,0:T(2,128)(2,1)} %copy.254), calls=%async_computation.3 | async-start | bytes 6291456 | tf_op jit(solution)/shard_map/all_to_all | solution.py:230
  132.5 0.2 fusion.170
  132.8 0.5 fusion.73
  133.3 0.8 copy.257
  134.0 38.4 %all-to-all-done.3 = bf16[128,3,2,2048]{3,2,1,0:T(2,128)(2,1)} async-done(((bf16[128,3,2,2048]{3,2,1,0:T(2,128)(2,1)}), bf16[128,3,2,2048]{3,2,1,0:T(2,128)(2,1)}, u32[]{:S(2)}, u32[]{:S(2)}) %all-to-all-start.3) | async-done | bytes 3145760 | tf_op jit(solution)/shard_map/all_to_all | solution.py:230
  172.4 3.9 %fusion.63 = f32[128,2048]{1,0:T(8,128)S(1)} fusion(bf16[128,3,2,2048]{3,2,1,0:T(2,128)(2,1)} %all-to-all-done.3, bf16[128,3,2,64]{0,3,2,1:T(8,128)(2,1)S(1)} %get-tuple-element.367, bf16[128,3,2,64]{0,3,2,1:T(8,128)(2,1)S(1)} %get-tuple-element.366), kind=kOutput, calls=%fused_computation.98 | convolution fusion | flops 403046400 | bytes 4390912 | tf_op jit(solution)/shard_map/dcet,dcex->tx/dot_general | solution.py:237
  176.3 0.8 fusion.117
  (74 shorter events, 3.0 us)
Async XLA Ops:
  0.6 10.9 %copy-start.3 = (s32[1,64,10]{1,0,2:T(1,128)S(1)}, s32[1,64,10]{1,0,2:T(1,128)}, u32[]{:S(2)}) copy-start(s32[1,64,10]{1,0,2:T(1,128)} %param.27) | copy-start | bytes 7684
  5.5 16.0 %all-to-all-start = ((bf16[8,66,512]{2,1,0:T(8,128)(2,1)}), bf16[8,66,512]{2,1,0:T(8,128)(2,1)S(1)}, u32[]{:S(2)}, u32[]{:S(2)}) async-start(bf16[8,66,512]{2,1,0:T(8,128)(2,1)} %pad_maximum_fusion), calls=%async_computation | async-start | bytes 1179648 | tf_op jit(solution)/shard_map/all_to_all | solution.py:111
  11.4 1.7 copy-start.1
  38.3 3.6 %copy-start.4 = (f32[128]{0:T(128)S(1)}, f32[128]{0:T(128)}, u32[]{:S(2)}) copy-start(f32[128]{0:T(128)} %param.23) | copy-start | bytes 1540
  39.4 7.8 %copy-start = (bf16[1,64,2048]{2,1,0:T(8,128)(2,1)S(1)}, bf16[1,64,2048]{2,1,0:T(8,128)(2,1)}, u32[]{:S(2)}) copy-start(bf16[1,64,2048]{2,1,0:T(8,128)(2,1)} %param.20) | copy-start | bytes 786436
  42.9 10.8 %all-to-all-start.1 = ((bf16[8,64,256]{2,1,0:T(8,128)(2,1)}), bf16[8,64,256]{2,1,0:T(8,128)(2,1)S(1)}, u32[]{:S(2)}, u32[]{:S(2)}) async-start(bf16[8,64,256]{2,1,0:T(8,128)(2,1)} %copy_bitcast_fusion), calls=%async_computation.1 | async-start | bytes 524288 | tf_op jit(solution)/shard_map/all_to_all | solution.py:192
  53.7 5.2 %copy-start.2 = (f32[2048]{0:T(1024)S(1)}, f32[2048]{0:T(1024)}, u32[]{:S(2)}) copy-start(f32[2048]{0:T(1024)} %param.26) | copy-start | bytes 24580
  112.9 6.7 %copy-start.5 = (bf16[2,512,2048]{2,1,0:T(8,128)(2,1)S(1)}, bf16[2,512,2048]{2,1,0:T(8,128)(2,1)}, u32[]{:S(2)}) copy-start(bf16[2,512,2048]{2,1,0:T(8,128)(2,1)} %param.30) | copy-start | bytes 12582916
  126.4 46.1 %all-to-all-start.3 = ((bf16[128,3,2,2048]{3,2,1,0:T(2,128)(2,1)}), bf16[128,3,2,2048]{3,2,1,0:T(2,128)(2,1)}, u32[]{:S(2)}, u32[]{:S(2)}) async-start(bf16[128,3,2,2048]{3,2,1,0:T(2,128)(2,1)} %copy.254), calls=%async_computation.3 | async-start | bytes 6291456 | tf_op jit(solution)/shard_map/all_to_all | solution.py:230

commit v4 on v3

--- a/solution.py
+++ b/solution.py
@@ -108,7 +108,23 @@
         ],
         axis=1,
     )
+    flat_ids = routes[0].reshape(-1)
+    onehot = (flat_ids[:, None] == jnp.arange(experts, dtype=jnp.int32)[None, :]).astype(jnp.int32)
+    earlier = jnp.cumsum(onehot, axis=0) - onehot
+    slot = jnp.sum(earlier * onehot, axis=1)
+    target = (flat_ids * cap + slot).reshape(seq, TOPK)
+    slots = (
+        jnp.arange(experts * cap, dtype=jnp.int32)
+        .reshape(n_dev, EXP_DEV, cap)
+        .transpose(0, 2, 1)
+    )
+    hits = target[None, None, None, :, :] == slots[..., None, None]
+    dispatch = jnp.sum(jnp.where(hits, 1.0, 0.0), axis=-1).astype(jnp.bfloat16)
+    scores = route_scores[0]
+    mix_weights = scores / jnp.sum(scores, axis=-1, keepdims=True)
+    combine = jnp.sum(jnp.where(hits, mix_weights, 0.0), axis=-1)
     got = lax.all_to_all(packed, "ctx", 0, 0, tiled=True)
+    got, dispatch, combine = lax.optimization_barrier((got, dispatch, combine))
     arrived = got[:, :seq]
     rd = (
         got[:, seq:]
@@ -202,18 +218,6 @@
         resid * lax.rsqrt(jnp.mean(resid * resid, axis=-1, keepdims=True) + 1e-06) * post_gain
     ).astype(jnp.bfloat16)
 
-    flat_ids = routes[0].reshape(-1)
-    onehot = (flat_ids[:, None] == jnp.arange(experts, dtype=jnp.int32)[None, :]).astype(jnp.int32)
-    earlier = jnp.cumsum(onehot, axis=0) - onehot
-    slot = jnp.sum(earlier * onehot, axis=1)
-    target = (flat_ids * cap + slot).reshape(seq, TOPK)
-    slots = (
-        jnp.arange(experts * cap, dtype=jnp.int32)
-        .reshape(n_dev, EXP_DEV, cap)
-        .transpose(0, 2, 1)
-    )
-    hits = target[None, None, None, :, :] == slots[..., None, None]
-    dispatch = jnp.sum(jnp.where(hits, 1.0, 0.0), axis=-1).astype(jnp.bfloat16)
     outgoing_rows = jnp.einsum(
         "dcet,tf->dcef", dispatch, moe_in, preferred_element_type=jnp.float32
     ).astype(jnp.bfloat16)
@@ -228,9 +232,6 @@
         "escf,efx->scex", inner, expert_down, preferred_element_type=jnp.float32
     ).astype(jnp.bfloat16)
     returned = lax.all_to_all(result, ("ctx", "req"), split_axis=0, concat_axis=0, tiled=True)
-    scores = route_scores[0]
-    mix_weights = scores / jnp.sum(scores, axis=-1, keepdims=True)
-    combine = jnp.sum(jnp.where(hits, mix_weights, 0.0), axis=-1)
     combine_hi = lax.reduce_precision(combine, exponent_bits=8, mantissa_bits=7)
     combine_lo = combine - combine_hi
     halves = jnp.concatenate([combine_hi, combine_lo], axis=-1).astype(jnp.bfloat16)

time: 178 us -> 186 us (1.045)
  matrix products: 35.1 us -> 41.8 us
  other arithmetic: 7.87 us -> 10.3 us
    dot_general x5, matrix products: 4.18 us -> 8.97 us  [level(): mc = jnp.einsum('...ij,...jk->...ik', inv, c, precision=highest)]
    unnamed x22 -> x26, local copies, waits for them, and re-layouts: 3.83 us -> 3.83 us
where the time goes in v4:
time: 186 us
  waiting for transfers between devices  51.9 us (28%)
  blocking collectives  49.7 us (27%)
  matrix products  41.8 us (22%)
  starting transfers between devices  15.6 us (8%)
  local copies, waits for them, and re-layouts  14 us (8%)
  other arithmetic  10.3 us (6%)
  between operations  1.9 us (1%)
    all_to_all x1, blocking collectives, shards(): lax.all_to_all(outgoing_rows, ('ctx', 'req'), split_axis=0, concat_axis=0...  49.7 us
    all_to_all x1, waiting for transfers between devices, shards(): lax.all_to_all(result, ('ctx', 'req'), split_axis=0, concat_axis=0, tiled...  38.4 us
    dot_general x5, matrix products, level(): mc = jnp.einsum('...ij,...jk->...ik', inv, c, precision=highest)  8.97 us
    all_to_all x1, waiting for transfers between devices, shards(): got = lax.all_to_all(packed, 'ctx', 0, 0, tiled=True)  7.08 us
    dot_general x1, matrix products, shards(): jnp.einsum('scex,exf->escf', arrived_rows, expert_gate_up, preferred_elem...  6.65 us
    all_to_all x1, waiting for transfers between devices, shards(): back = lax.all_to_all(shaped, 'ctx', 0, 0, tiled=True)  6.44 us
    all_to_all x1, starting transfers between devices, shards(): got = lax.all_to_all(packed, 'ctx', 0, 0, tiled=True)  5.96 us
    all_to_all x1, starting transfers between devices, shards(): lax.all_to_all(result, ('ctx', 'req'), split_axis=0, concat_axis=0, tiled...  5.4 us
  transfers between devices with their start and end apart: 3, of which 3 were waited for; matrix products, arithmetic and copies ran while one was open for 2% of the time, Pallas kernels for 0%

profile of v4, /device:TPU:1, one launch (start us, length us, event | category | flops | bytes accessed | tf_op | source)
XLA Modules:
  0.0 185.7 jit_solution(15969133924039896675)
XLA Ops:
  0.6 0.7 pad_maximum_fusion.2
  1.6 1.0 copy.284
  2.6 0.9 copy.282
  3.6 0.9 copy.283
  4.6 0.9 pad_maximum_fusion
  5.5 6.0 %all-to-all-start = ((bf16[8,66,512]{2,1,0:T(8,128)(2,1)}), bf16[8,66,512]{2,1,0:T(8,128)(2,1)S(1)}, u32[]{:S(2)}, u32[]{:S(2)}) async-start(bf16[8,66,512]{2,1,0:T(8,128)(2,1)} %pad_maximum_fusion), calls=%async_computation | async-start | bytes 1179648 | tf_op jit(solution)/shard_map/all_to_all | solution.py:126
  12.0 0.2 fusion.79
  12.3 0.2 copy.224
  12.5 0.3 fusion.83
  13.1 1.1 fusion.68
  14.4 7.1 %all-to-all-done = bf16[8,66,512]{2,1,0:T(8,128)(2,1)S(1)} async-done(((bf16[8,66,512]{2,1,0:T(8,128)(2,1)}), bf16[8,66,512]{2,1,0:T(8,128)(2,1)S(1)}, u32[]{:S(2)}, u32[]{:S(2)}) %all-to-all-start) | async-done | bytes 540704 | tf_op jit(solution)/shard_map/all_to_all | solution.py:126
  21.5 0.2 fusion.106
  21.9 1.4 fusion.157
  23.5 0.5 reduce_window_sum.28
  23.9 0.2 slice_reduce_fusion.1
  24.2 0.2 slice_reduce_fusion
  24.3 1.0 broadcast_multiply_fusion
  25.3 1.2 select_subtract_fusion
  26.5 1.8 fusion.101
  28.3 0.7 convolution_subtract_fusion.2
  29.0 11.6 %while.18 = (s32[]{:T(128)}, f32[2,8,64,64]{3,2,1,0:T(8,128)S(1)}, f32[2,8,64]{2,1,0:T(8,128)S(1)}, pred[64,64]{1,0:T(8,128)(4,1)S(1)}, f32[8,64,64]{2,1,0:T(8,1...) while((s32[]{:T(128)}, f32[2,8,64,64]{3,2,1,0:T(8,128)S(1)}, ...), condition=%wide.region_9.10_spmd.clone.clone, body=%wide.region_8.9_spmd.clone.clone.sunk | while | flops 202275840 | bytes 2935545 | solution.py:40
  29.1 0.1 fusion.224
  29.3 1.8 fusion.225
  31.1 0.7 convolution_subtract_fusion.12
  31.9 0.1 fusion.226
  32.2 1.8 fusion.227
  34.0 0.7 convolution_subtract_fusion.13
  34.8 0.1 fusion.224
  35.0 1.8 fusion.225
  36.8 0.7 convolution_subtract_fusion.12
  37.6 0.1 fusion.226
  37.9 1.8 fusion.227
  39.7 0.7 convolution_subtract_fusion.13
  40.5 0.2 bitcast_multiply_fusion.3
  40.7 0.3 slice_reduce_fusion.2
  41.0 2.1 %fusion.74 = f32[2,8,64,256]{3,2,1,0:T(8,128)S(1)} fusion(f32[2,8,64,64]{3,2,1,0:T(8,128)S(1)} %get-tuple-element.255, f32[2,8,64,128]{3,2,1,0:T(8,128)} %broadcast_multiply_fusion, f32[2,8,64,128]{3,2,1,0:T(8,128)S(1)} %bitcast_bitcast_fusion), kind=kOutput, calls=%fused_computation.118 | convolution fusion | flops 201588736 | bytes 2359296 | tf_op jit(solution)/shard_map/hnts,hnsf->hntf/dot_general | solution.py:159
  43.1 1.9 %fusion.180 = f32[16,128,256]{2,1,0:T(8,128)S(1)} fusion(f32[16,64,128]{2,1,0:T(8,128)S(1)} %bitcast_multiply_fusion.3, f32[16,64,256]{2,1,0:T(8,128)S(1)} %bitcast.413), kind=kOutput, calls=%fused_computation.325 | convolution fusion | flops 402653184 | bytes 3670016 | tf_op jit(solution)/shard_map/btd,btf->bdf/dot_general | solution.py:164
  45.0 0.3 bitcast_dynamic-update-slice_fusion.5
  45.2 0.3 bitcast_dynamic-update-slice_fusion.4
  45.5 0.3 bitcast_dynamic-update-slice_fusion.3
  45.8 0.3 bitcast_dynamic-update-slice_fusion.2
  46.1 0.3 bitcast_dynamic-update-slice_fusion.1
  46.4 0.3 fusion.71
  46.6 1.1 convolution_subtract_fusion.3
  47.7 0.8 fusion.111
  48.5 0.7 fusion.108
  49.2 1.0 fusion.93
  50.2 1.0 copy_bitcast_fusion
  51.3 4.3 %all-to-all-start.1 = ((bf16[8,64,256]{2,1,0:T(8,128)(2,1)}), bf16[8,64,256]{2,1,0:T(8,128)(2,1)S(1)}, u32[]{:S(2)}, u32[]{:S(2)}) async-start(bf16[8,64,256]{2,1,0:T(8,128)(2,1)} %copy_bitcast_fusion), calls=%async_computation.1 | async-start | bytes 524288 | tf_op jit(solution)/shard_map/all_to_all | solution.py:208
  55.6 6.4 %all-to-all-done.1 = bf16[8,64,256]{2,1,0:T(8,128)(2,1)S(1)} async-done(((bf16[8,64,256]{2,1,0:T(8,128)(2,1)}), bf16[8,64,256]{2,1,0:T(8,128)(2,1)S(1)}, u32[]{:S(2)}, u32[]{:S(2)}) %all-to-all-start.1) | async-done | bytes 262176 | tf_op jit(solution)/shard_map/all_to_all | solution.py:208
  62.1 5.2 %multiply_reduce_fusion = (f32[64]{0:T(128)S(1)}, f32[64,2048]{1,0:T(8,128)S(1)}) fusion(bf16[8,256,2048]{2,1,0:T(8,128)(2,1)} %bitcast.412, f32[64,8,256]{2,1,0:T(8,128)S(1)} %bitcast.421, bf16[8,64,256]{2,1,0:T(8,128)(2,1)S(1)} %all-to-all-done.1, bf16[1,64,2048]{2,1,0:T(8,128)(2,1)} %param.25), kind=kOutput, calls=%fused_computation.156 | convolution fusion | flops 538312640 | bytes 9961728 | tf_op jit(solution)/shard_map/jtf,jfd->td/dot_general | solution.py:211
  67.3 1.0 convolution_convert_fusion
  68.3 3.2 %copy.251 = bf16[128,3,2,2048]{3,2,1,0:T(2,128)(2,1)S(1)} copy(bf16[128,3,2,2048]{3,0,1,2:T(8,128)(2,1)S(1)} %convolution_convert_fusion) | data formatting | bytes 6291456 | tf_op jit(solution)/shard_map/convert_element_type | solution.py:223
  71.6 49.7 %all_to_all.20 = bf16[128,3,2,2048]{3,2,1,0:T(2,128)(2,1)S(1)} all-to-all(bf16[128,3,2,2048]{3,2,1,0:T(2,128)(2,1)S(1)} %copy.251), channel_id=1, replica_groups=mesh['ctx'=8,'req'=16] {'ctx','req'}, dimensions={0} | all-to-all | bytes 6291456 | tf_op jit(solution)/shard_map/all_to_all | solution.py:224
  121.3 6.6 %fusion.50 = f32[2,128,3,1024]{3,1,2,0:T(8,128)S(1)} fusion(bf16[2,2048,1024]{2,1,0:T(8,128)(2,1)} %param.29, bf16[128,3,2,2048]{3,2,1,0:T(2,128)(2,1)S(1)} %all_to_all.20), kind=kOutput, calls=%fused_computation.86 | convolution fusion | flops 3221225472 | bytes 14680064 | tf_op jit(solution)/shard_map/scex,exf->escf/dot_general | solution.py:227
  128.0 1.9 %fusion.60 = bf16[128,3,2,2048]{3,0,2,1:T(8,128)(2,1)S(1)} fusion(bf16[2,512,2048]{2,1,0:T(8,128)(2,1)S(1)} %copy-done.7, f32[2,128,3,1024]{3,1,2,0:T(8,128)S(1)} %fusion.50), kind=kOutput, calls=%fused_computation.95 | convolution fusion | flops 1614544896 | bytes 10485760 | tf_op jit(solution)/shard_map/escf,efx->scex/dot_general | solution.py:231
  129.9 4.9 %copy.254 = bf16[128,3,2,2048]{3,2,1,0:T(2,128)(2,1)} copy(bf16[128,3,2,2048]{3,0,2,1:T(8,128)(2,1)S(1)} %fusion.60) | data formatting | bytes 6291456 | tf_op jit(solution)/shard_map/convert_element_type | solution.py:233
  134.8 5.4 %all-to-all-start.3 = ((bf16[128,3,2,2048]{3,2,1,0:T(2,128)(2,1)}), bf16[128,3,2,2048]{3,2,1,0:T(2,128)(2,1)}, u32[]{:S(2)}, u32[]{:S(2)}) async-start(bf16[128,3,2,2048]{3,2,1,0:T(2,128)(2,1)} %copy.254), calls=%async_computation.3 | async-start | bytes 6291456 | tf_op jit(solution)/shard_map/all_to_all | solution.py:234
  141.0 0.2 fusion.170
  141.3 0.5 fusion.73
  141.8 0.8 copy.257
  142.6 38.4 %all-to-all-done.3 = bf16[128,3,2,2048]{3,2,1,0:T(2,128)(2,1)} async-done(((bf16[128,3,2,2048]{3,2,1,0:T(2,128)(2,1)}), bf16[128,3,2,2048]{3,2,1,0:T(2,128)(2,1)}, u32[]{:S(2)}, u32[]{:S(2)}) %all-to-all-start.3) | async-done | bytes 3145760 | tf_op jit(solution)/shard_map/all_to_all | solution.py:234
  181.0 3.9 %fusion.63 = f32[128,2048]{1,0:T(8,128)S(1)} fusion(bf16[128,3,2,2048]{3,2,1,0:T(2,128)(2,1)} %all-to-all-done.3, bf16[128,3,2,64]{0,3,2,1:T(8,128)(2,1)S(1)} %get-tuple-element.373, bf16[128,3,2,64]{0,3,2,1:T(8,128)(2,1)S(1)} %get-tuple-element.372), kind=kOutput, calls=%fused_computation.98 | convolution fusion | flops 403046400 | bytes 4390912 | tf_op jit(solution)/shard_map/dcet,dcex->tx/dot_general | solution.py:238
  184.9 0.8 fusion.117
  (78 shorter events, 3.0 us)
Async XLA Ops:
  0.6 10.8 %copy-start.5 = (s32[1,64,10]{1,0,2:T(1,128)S(1)}, s32[1,64,10]{1,0,2:T(1,128)}, u32[]{:S(2)}) copy-start(s32[1,64,10]{1,0,2:T(1,128)} %param.27) | copy-start | bytes 7684
  5.5 16.0 %all-to-all-start = ((bf16[8,66,512]{2,1,0:T(8,128)(2,1)}), bf16[8,66,512]{2,1,0:T(8,128)(2,1)S(1)}, u32[]{:S(2)}, u32[]{:S(2)}) async-start(bf16[8,66,512]{2,1,0:T(8,128)(2,1)} %pad_maximum_fusion), calls=%async_computation | async-start | bytes 1179648 | tf_op jit(solution)/shard_map/all_to_all | solution.py:126
  11.4 1.6 copy-start.3
  46.6 3.6 %copy-start.6 = (f32[128]{0:T(128)S(1)}, f32[128]{0:T(128)}, u32[]{:S(2)}) copy-start(f32[128]{0:T(128)} %param.23) | copy-start | bytes 1540
  47.7 7.9 %copy-start.2 = (bf16[1,64,2048]{2,1,0:T(8,128)(2,1)S(1)}, bf16[1,64,2048]{2,1,0:T(8,128)(2,1)}, u32[]{:S(2)}) copy-start(bf16[1,64,2048]{2,1,0:T(8,128)(2,1)} %param.20) | copy-start | bytes 786436
  51.3 10.8 %all-to-all-start.1 = ((bf16[8,64,256]{2,1,0:T(8,128)(2,1)}), bf16[8,64,256]{2,1,0:T(8,128)(2,1)S(1)}, u32[]{:S(2)}, u32[]{:S(2)}) async-start(bf16[8,64,256]{2,1,0:T(8,128)(2,1)} %copy_bitcast_fusion), calls=%async_computation.1 | async-start | bytes 524288 | tf_op jit(solution)/shard_map/all_to_all | solution.py:208
  62.1 5.2 %copy-start.1 = (bf16[128,3,2,64]{0,3,2,1:T(8,128)(2,1)S(1)}, bf16[128,3,2,64]{0,3,2,1:T(8,128)(2,1)}, u32[]{:S(2)}) copy-start(bf16[128,3,2,64]{0,3,2,1:T(8,128)(2,1)} %get-tuple-element.257) | copy-start | bytes 294916
  62.1 5.2 %copy-start.4 = (f32[2048]{0:T(1024)S(1)}, f32[2048]{0:T(1024)}, u32[]{:S(2)}) copy-start(f32[2048]{0:T(1024)} %param.26) | copy-start | bytes 24580
  121.3 6.7 %copy-start.7 = (bf16[2,512,2048]{2,1,0:T(8,128)(2,1)S(1)}, bf16[2,512,2048]{2,1,0:T(8,128)(2,1)}, u32[]{:S(2)}) copy-start(bf16[2,512,2048]{2,1,0:T(8,128)(2,1)} %param.30) | copy-start | bytes 12582916
  134.8 7.8 %copy-start = (f32[128,3,2,64]{0,3,2,1:T(8,128)S(1)}, f32[128,3,2,64]{0,3,2,1:T(8,128)}, u32[]{:S(2)}) copy-start(f32[128,3,2,64]{0,3,2,1:T(8,128)} %get-tuple-element.256) | copy-start | bytes 589828
  134.8 46.2 %all-to-all-start.3 = ((bf16[128,3,2,2048]{3,2,1,0:T(2,128)(2,1)}), bf16[128,3,2,2048]{3,2,1,0:T(2,128)(2,1)}, u32[]{:S(2)}, u32[]{:S(2)}) async-start(bf16[128,3,2,2048]{3,2,1,0:T(2,128)(2,1)} %copy.254), calls=%async_computation.3 | async-start | bytes 6291456 | tf_op jit(solution)/shard_map/all_to_all | solution.py:234
